TPU v7x, 512 devices: a whole 4x4x16 slice. The times are simulated.
512 devices in a mesh: wide: 32 (over y, x, core), grp: 16 (over z).
Axes of the slice: x: 4, y: 4, z: 16, core: 2. Of those that a mesh axis runs over, the one named last changes fastest.
Arguments:
- embeds: bfloat16 [147456, 1024], P(('wide', 'grp')), may hold values from -700 to 700
- bucket: int32 [147456], P(('wide', 'grp')), may hold values from 0 to 31, as said below
- pairs: int32 [8192], P(('wide', 'grp')), may hold values from -1 to 15, as said below
Outputs:
- density: float32 [512, 384], P(('wide', 'grp'))
Inputs may be any that keep to these rules, and one draw needn't show every extreme that they name: At most 12 rows of one file shard name the same bucket; for every g some bucket is named by exactly 12 rows of every shard (s, g). `pairs`: the 16 entries of block (o, g) name distinct blocks (o, b) by b, live entries first and -1 after; for every o some block has all 16 entries live.
All inputs are finite; a program needn't handle non-finite values.
Results may differ from a plain program's by a relative error of at most 0.0034.
Values may be sent and summed in bfloat16 or wider, within the bound.
No kernel may reach another device: no remote copies, remote signals or barrier semaphores. Data moves between devices by JAX's collectives and lax.ppermute only.
A program may use at most 64 MiB of HBM per device.

v0:
```python
import jax
import jax.numpy as jnp
import numpy as np
from jax import lax
from jax.sharding import PartitionSpec as P


BLK = 384


SHARPNESS = 10.0
EPSILON = 1e-06
SENTINEL = 2.0


def pair_products(left_rows, right_rows):
    cosines = lax.dot_general(
        left_rows, right_rows, (((1,), (1,)), ((), ())), preferred_element_type=jnp.float32
    )
    return jnp.exp(SHARPNESS * (cosines - 1.0))


def per_device(embeds, bucket, pairs):
    wide_count = lax.axis_size("wide")
    grp_count = lax.axis_size("grp")
    feature_width = embeds.shape[1]
    capacity = BLK // wide_count
    me = lax.axis_index("grp")

    blocks_iota = jnp.arange(grp_count, dtype=jnp.int32)
    relative = (pairs - me) % grp_count
    near = jnp.any(
        (relative[:, None] == blocks_iota[None, :]) & (pairs >= 0)[:, None], axis=0
    ).astype(jnp.float32)

    floats = embeds.astype(jnp.float32)
    unit_rows = (
        floats * lax.rsqrt(jnp.sum(floats * floats, axis=1, keepdims=True) + EPSILON)
    ).astype(jnp.bfloat16)
    onehot = (bucket[:, None] == jnp.arange(wide_count, dtype=jnp.int32)[None, :]).astype(jnp.int32)
    row_ranks = jnp.sum(jnp.cumsum(onehot, axis=0) * onehot, axis=1) - 1
    send_slots = bucket * capacity + row_ranks
    sentinel_row = jnp.where(jnp.arange(feature_width) == 0, SENTINEL, 0.0).astype(jnp.float32)
    parts = 3
    split = capacity // parts
    halves = []
    for h in range(parts):
        slot_ids = (
            jnp.arange(wide_count, dtype=jnp.int32)[:, None] * capacity
            + h * split
            + jnp.arange(split, dtype=jnp.int32)[None, :]
        ).reshape(-1)
        hits = slot_ids[:, None] == send_slots[None, :]
        placed_rows = lax.dot_general(
            hits.astype(jnp.bfloat16), unit_rows, (((1,), (0,)), ((), ())),
            preferred_element_type=jnp.float32,
        )
        filled = jnp.any(hits, axis=1)
        part = jnp.where(filled[:, None], placed_rows, sentinel_row[None, :]).astype(jnp.bfloat16)
        halves.append(part.reshape(wide_count, split, feature_width))
    own_halves = [
        lax.all_to_all(h, "wide", split_axis=0, concat_axis=0, tiled=True).reshape(-1, feature_width)
        for h in halves
    ]

    def valid_of(rows):
        return (rows[:, 0].astype(jnp.float32) < 1.5).astype(jnp.float32)

    def shift(value, offset):
        return lax.ppermute(
            value, "grp", [(i, (i + offset) % grp_count) for i in range(grp_count)]
        )

    reach = 4
    rows_at = {}
    for part in own_halves:
        left = part
        right = part
        rows_at.setdefault(0, []).append(part)
        for step in range(1, reach + 1):
            left = shift(left, 1)
            right = shift(right, -1)
            rows_at.setdefault(-step, []).append(left)
            rows_at.setdefault(step, []).append(right)
    halves_at = rows_at
    rows_at = {}
    valid_at = {}
    for k, v in halves_at.items():
        rows_at[k] = jnp.concatenate(v, axis=0)
        valid_at[k] = valid_of(rows_at[k])
    own = rows_at[0]

    early = {}
    late = {}

    def add(sums_by_target, target, source, sums):
        sums_by_target.setdefault(target, []).append((source, sums))

    e = pair_products(own, own)
    add(early, 0, 0, jnp.sum(e * valid_at[0][None, :], axis=1))
    plan = [(0, 1), (0, 2), (0, 3), (-2, 2), (-2, 3), (-3, 3), (-4, 3)]
    for p, q in plan:
        e = pair_products(rows_at[p], rows_at[q])
        to_p = jnp.sum(e * valid_at[q][None, :], axis=1)
        to_q = jnp.sum(e * valid_at[p][:, None], axis=0)
        group = late if max(-p, q) == reach else early
        add(group, p, q, to_p)
        add(group, q, p, to_q)
    e = pair_products(rows_at[-reach], rows_at[reach])
    add(late, -reach, reach, jnp.sum(e * valid_at[reach][None, :], axis=1))

    def near_at(offsets):
        hits = (np.asarray(offsets)[..., None] % grp_count) == np.arange(grp_count)
        return jnp.sum(jnp.asarray(hits, jnp.float32) * near, axis=-1)

    def weighted(stacked, items, target):
        weights = near_at([s - target for s, _ in items])
        return jnp.sum(stacked * weights[:, None], axis=0)

    slot_sums = weighted(jnp.stack([s for _, s in early[0]]), early[0], 0)

    depth = max(len(items) for t, items in early.items() if t != 0)
    zero = jnp.zeros((BLK,), jnp.float32)
    table = [[zero] * depth for _ in range(grp_count)]
    source_table = [[0] * depth for _ in range(grp_count)]
    present_table = [[0.0] * depth for _ in range(grp_count)]
    for target, items in early.items():
        if target == 0:
            continue
        for k, (source, sums) in enumerate(items):
            table[target % grp_count][k] = sums
            source_table[target % grp_count][k] = source - target
            present_table[target % grp_count][k] = 1.0
    by_offset = jnp.stack([jnp.stack(row) for row in table])
    start = (grp_count - me) % grp_count
    by_device = lax.dynamic_slice_in_dim(
        jnp.concatenate([by_offset, by_offset], axis=0), start, grp_count, 0
    )
    arrived_sums = lax.all_to_all(by_device, "grp", split_axis=0, concat_axis=0, tiled=True)
    gap_order = [(-g) % grp_count for g in range(grp_count)]
    by_gap = near_at(np.asarray(source_table)[gap_order]) * jnp.asarray(
        np.asarray(present_table, np.float32)[gap_order]
    )
    weights = lax.dynamic_slice_in_dim(jnp.concatenate([by_gap, by_gap], axis=0), start, grp_count, 0)
    slot_sums = slot_sums + jnp.sum(arrived_sums * weights[:, :, None], axis=(0, 1))

    for target, items in sorted(late.items()):
        stacked = shift(jnp.stack([s for _, s in items]), target)
        slot_sums = slot_sums + weighted(stacked, items, target)

    own_valid = valid_at[0].reshape(parts, wide_count, split).transpose(1, 0, 2).reshape(wide_count, capacity)
    arrived = jnp.sum(own_valid, axis=1).astype(jnp.int32)
    offsets = jnp.cumsum(arrived) - arrived
    within = jnp.arange(capacity, dtype=jnp.int32)
    places = jnp.where(own_valid > 0, offsets[:, None] + within[None, :], BLK)
    places = places.reshape(wide_count, parts, split).transpose(1, 0, 2).reshape(-1)
    rows_iota = jnp.arange(BLK, dtype=jnp.int32)
    density = jnp.sum(jnp.where(places[:, None] == rows_iota[None, :], slot_sums[:, None], 0.0), axis=0)
    return density.reshape(1, BLK)


def solution(mesh):
    placed = (P(("wide", "grp"), None), P(("wide", "grp")), P(("wide", "grp")))
    return jax.shard_map(per_device, mesh=mesh, in_specs=placed, out_specs=P(("wide", "grp"), None), check_vma=False)
```

profile of v0, /device:TPU:6, one launch (start us, length us, event | category | flops | bytes accessed | tf_op | source)
XLA Modules:
  0.0 169.5 jit_solution(14459779161723620758)
XLA Ops:
  5.4 9.4 %all-to-all-start.1 = ((bf16[32,4,1024]{2,1,0:T(4,128)(2,1)}), bf16[32,4,1024]{2,1,0:T(4,128)(2,1)S(1)}, u32[]{:S(2)}, u32[]{:S(2)}) async-start(bf16[32,4,1024]{2,1,0:T(4,128)(2,1)} %reshape.252), calls=%async_computation.1 | async-start | bytes 524288 | tf_op jit(solution)/shard_map/all_to_all | solution.py:62
  17.0 5.0 %all-to-all-done.1 = bf16[32,4,1024]{2,1,0:T(4,128)(2,1)S(1)} async-done(((bf16[32,4,1024]{2,1,0:T(4,128)(2,1)}), bf16[32,4,1024]{2,1,0:T(4,128)(2,1)S(1)}, u32[]{:S(2)}, u32[]{:S(2)}) %all-to-all-start.1) | async-done | bytes 262176 | tf_op jit(solution)/shard_map/all_to_all | solution.py:62
  22.0 5.6 %all-to-all-start = ((bf16[32,4,1024]{2,1,0:T(4,128)(2,1)}), bf16[32,4,1024]{2,1,0:T(4,128)(2,1)S(1)}, u32[]{:S(2)}, u32[]{:S(2)}) async-start(bf16[32,4,1024]{2,1,0:T(4,128)(2,1)} %reshape.250), calls=%async_computation | async-start | bytes 524288 | tf_op jit(solution)/shard_map/all_to_all | solution.py:62
  29.0 5.6 %all-to-all-done = bf16[32,4,1024]{2,1,0:T(4,128)(2,1)S(1)} async-done(((bf16[32,4,1024]{2,1,0:T(4,128)(2,1)}), bf16[32,4,1024]{2,1,0:T(4,128)(2,1)S(1)}, u32[]{:S(2)}, u32[]{:S(2)}) %all-to-all-start) | async-done | bytes 262176 | tf_op jit(solution)/shard_map/all_to_all | solution.py:62
  34.6 5.6 %all-to-all-start.2 = ((bf16[32,4,1024]{2,1,0:T(4,128)(2,1)}), bf16[32,4,1024]{2,1,0:T(4,128)(2,1)S(1)}, u32[]{:S(2)}, u32[]{:S(2)}) async-start(bf16[32,4,1024]{2,1,0:T(4,128)(2,1)} %reshape.254), calls=%async_computation.2 | async-start | bytes 524288 | tf_op jit(solution)/shard_map/all_to_all | solution.py:62
  42.5 9.5 %collective-permute-start = (bf16[128,1024]{1,0:T(8,128)(2,1)S(1)}, bf16[128,1024]{1,0:T(8,128)(2,1)S(1)}, u32[]{:S(2)}, u32[]{:S(2)}) collective-permute-start(bf16[128,1024]{1,0:T(8,128)(2,1)S(1)} %reshape.251), channel_id=1, source_target_pairs={{0,15},{1,0},{2,1},{3,2},{4,3},{5,4},{6,5},{7,6},{8,7},{9,8},{10,9... | collective-permute-start | bytes 786440 | tf_op jit(solution)/shard_map/ppermute | solution.py:70
  54.1 5.1 %collective-permute-start.1 = (bf16[128,1024]{1,0:T(8,128)(2,1)S(1)}, bf16[128,1024]{1,0:T(8,128)(2,1)S(1)}, u32[]{:S(2)}, u32[]{:S(2)}) collective-permute-start(bf16[128,1024]{1,0:T(8,128)(2,1)S(1)} %reshape.253), channel_id=1, source_target_pairs={{0,15},{1,0},{2,1},{3,2},{4,3},{5,4},{6,5},{7,6},{8,7},{9,8},{10,9... | collective-permute-start | bytes 786440 | tf_op jit(solution)/shard_map/ppermute | solution.py:70
  59.3 2.7 %collective-permute-start.2 = (bf16[128,1024]{1,0:T(8,128)(2,1)S(1)}, bf16[128,1024]{1,0:T(8,128)(2,1)S(1)}, u32[]{:S(2)}, u32[]{:S(2)}) collective-permute-start(bf16[128,1024]{1,0:T(8,128)(2,1)S(1)} %reshape.255), channel_id=1, source_target_pairs={{0,15},{1,0},{2,1},{3,2},{4,3},{5,4},{6,5},{7,6},{8,7},{9,8},{10,9... | collective-permute-start | bytes 786440 | tf_op jit(solution)/shard_map/ppermute | solution.py:70
  63.6 3.1 %collective-permute-start.13 = (bf16[128,1024]{1,0:T(8,128)(2,1)S(1)}, bf16[128,1024]{1,0:T(8,128)(2,1)S(1)}, u32[]{:S(2)}, u32[]{:S(2)}) collective-permute-start(bf16[128,1024]{1,0:T(8,128)(2,1)S(1)} %reshape.255), channel_id=1, source_target_pairs={{0,1},{1,2},{2,3},{3,4},{4,5},{5,6},{6,7},{7,8},{8,9},{9,10},{10,1... | collective-permute-start | bytes 786440 | tf_op jit(solution)/shard_map/ppermute | solution.py:70
  66.7 3.9 %collective-permute-start.3 = (bf16[128,1024]{1,0:T(8,128)(2,1)S(1)}, bf16[128,1024]{1,0:T(8,128)(2,1)S(1)}, u32[]{:S(2)}, u32[]{:S(2)}) collective-permute-start(bf16[128,1024]{1,0:T(8,128)(2,1)S(1)} %collective-permute-done), channel_id=1, source_target_pairs={{0,15},{1,0},{2,1},{3,2},{4,3},{5,4},{6,5},{7,6},{8,7},{9,8},{10,9... | collective-permute-start | bytes 786440 | tf_op jit(solution)/shard_map/ppermute | solution.py:70
  73.3 5.1 %collective-permute-start.4 = (bf16[128,1024]{1,0:T(8,128)(2,1)S(1)}, bf16[128,1024]{1,0:T(8,128)(2,1)S(1)}, u32[]{:S(2)}, u32[]{:S(2)}) collective-permute-start(bf16[128,1024]{1,0:T(8,128)(2,1)S(1)} %collective-permute-done.1), channel_id=1, source_target_pairs={{0,15},{1,0},{2,1},{3,2},{4,3},{5,4},{6,5},{7,6},{8,7},{9,8},{10,9... | collective-permute-start | bytes 786440 | tf_op jit(solution)/shard_map/ppermute | solution.py:70
  80.5 3.9 %collective-permute-start.12 = (bf16[128,1024]{1,0:T(8,128)(2,1)S(1)}, bf16[128,1024]{1,0:T(8,128)(2,1)S(1)}, u32[]{:S(2)}, u32[]{:S(2)}) collective-permute-start(bf16[128,1024]{1,0:T(8,128)(2,1)S(1)} %collective-permute-done.11), channel_id=1, source_target_pairs={{0,1},{1,2},{2,3},{3,4},{4,5},{5,6},{6,7},{7,8},{8,9},{9,10},{10,1... | collective-permute-start | bytes 786440 | tf_op jit(solution)/shard_map/ppermute | solution.py:70
  86.4 5.1 %collective-permute-start.6 = (bf16[128,1024]{1,0:T(8,128)(2,1)S(1)}, bf16[128,1024]{1,0:T(8,128)(2,1)S(1)}, u32[]{:S(2)}, u32[]{:S(2)}) collective-permute-start(bf16[128,1024]{1,0:T(8,128)(2,1)S(1)} %collective-permute-done.3), channel_id=1, source_target_pairs={{0,15},{1,0},{2,1},{3,2},{4,3},{5,4},{6,5},{7,6},{8,7},{9,8},{10,9... | collective-permute-start | bytes 786440 | tf_op jit(solution)/shard_map/ppermute | solution.py:70
  93.4 2.2 %collective-permute-done.14 = bf16[128,1024]{1,0:T(8,128)(2,1)S(1)} collective-permute-done((bf16[128,1024]{1,0:T(8,128)(2,1)S(1)}, bf16[128,1024]{1,0:T(8,128)(2,1)S(1)}, u32[]{:S(2)}, u32[]{:S(2)}) %collective-permute-start.14) | collective-permute-done | bytes 262176 | tf_op jit(solution)/shard_map/ppermute | solution.py:70
  98.3 5.1 %collective-permute-start.7 = (bf16[128,1024]{1,0:T(8,128)(2,1)S(1)}, bf16[128,1024]{1,0:T(8,128)(2,1)S(1)}, u32[]{:S(2)}, u32[]{:S(2)}) collective-permute-start(bf16[128,1024]{1,0:T(8,128)(2,1)S(1)} %collective-permute-done.4), channel_id=1, source_target_pairs={{0,15},{1,0},{2,1},{3,2},{4,3},{5,4},{6,5},{7,6},{8,7},{9,8},{10,9... | collective-permute-start | bytes 786440 | tf_op jit(solution)/shard_map/ppermute | solution.py:70
  107.4 5.1 %collective-permute-start.8 = (bf16[128,1024]{1,0:T(8,128)(2,1)S(1)}, bf16[128,1024]{1,0:T(8,128)(2,1)S(1)}, u32[]{:S(2)}, u32[]{:S(2)}) collective-permute-start(bf16[128,1024]{1,0:T(8,128)(2,1)S(1)} %collective-permute-done.5), channel_id=1, source_target_pairs={{0,15},{1,0},{2,1},{3,2},{4,3},{5,4},{6,5},{7,6},{8,7},{9,8},{10,9... | collective-permute-start | bytes 786440 | tf_op jit(solution)/shard_map/ppermute | solution.py:70
  112.6 3.9 %collective-permute-start.21 = (bf16[128,1024]{1,0:T(8,128)(2,1)S(1)}, bf16[128,1024]{1,0:T(8,128)(2,1)S(1)}, u32[]{:S(2)}, u32[]{:S(2)}) collective-permute-start(bf16[128,1024]{1,0:T(8,128)(2,1)S(1)} %collective-permute-done.6), channel_id=1, source_target_pairs={{0,15},{1,0},{2,1},{3,2},{4,3},{5,4},{6,5},{7,6},{8,7},{9,8},{10,9... | collective-permute-start | bytes 786440 | tf_op jit(solution)/shard_map/ppermute | solution.py:70
  122.1 5.6 %collective-permute-start.22 = (bf16[128,1024]{1,0:T(8,128)(2,1)S(1)}, bf16[128,1024]{1,0:T(8,128)(2,1)S(1)}, u32[]{:S(2)}, u32[]{:S(2)}) collective-permute-start(bf16[128,1024]{1,0:T(8,128)(2,1)S(1)} %collective-permute-done.7), channel_id=1, source_target_pairs={{0,15},{1,0},{2,1},{3,2},{4,3},{5,4},{6,5},{7,6},{8,7},{9,8},{10,9... | collective-permute-start | bytes 786440 | tf_op jit(solution)/shard_map/ppermute | solution.py:70
  131.7 5.3 %collective-permute-start.23 = (bf16[128,1024]{1,0:T(8,128)(2,1)S(1)}, bf16[128,1024]{1,0:T(8,128)(2,1)S(1)}, u32[]{:S(2)}, u32[]{:S(2)}) collective-permute-start(bf16[128,1024]{1,0:T(8,128)(2,1)S(1)} %collective-permute-done.8), channel_id=1, source_target_pairs={{0,15},{1,0},{2,1},{3,2},{4,3},{5,4},{6,5},{7,6},{8,7},{9,8},{10,9... | collective-permute-start | bytes 786440 | tf_op jit(solution)/shard_map/ppermute | solution.py:70
  137.1 3.6 %collective-permute-done.23 = bf16[128,1024]{1,0:T(8,128)(2,1)S(1)} collective-permute-done((bf16[128,1024]{1,0:T(8,128)(2,1)S(1)}, bf16[128,1024]{1,0:T(8,128)(2,1)S(1)}, u32[]{:S(2)}, u32[]{:S(2)}) %collective-permute-start.23) | collective-permute-done | bytes 262176 | tf_op jit(solution)/shard_map/ppermute | solution.py:70
  144.0 9.5 %all-to-all-start.3 = ((f32[16,3,384]{2,1,0:T(4,128)}), f32[16,3,384]{2,1,0:T(4,128)S(1)}, u32[]{:S(2)}, u32[]{:S(2)}) async-start(f32[16,3,384]{2,1,0:T(4,128)} %constant_dynamic-slice_fusion.1), calls=%async_computation.3 | async-start | bytes 196608 | tf_op jit(solution)/shard_map/all_to_all | solution.py:139
  153.5 5.6 %collective-permute-start.25 = (f32[1,384]{1,0:T(1,128)S(1)}, f32[1,384]{1,0:T(1,128)S(1)}, u32[]{:S(2)}, u32[]{:S(2)}) collective-permute-start(f32[1,384]{1,0:T(1,128)S(1)} %stack.116), channel_id=1, source_target_pairs={{0,3},{1,4},{2,5},{3,6},{4,7},{5,8},{6,9},{7,10},{8,11},{9,12},{10... | collective-permute-start | bytes 4616 | tf_op jit(solution)/shard_map/ppermute | solution.py:70
  159.1 4.6 %collective-permute-start.24 = (f32[2,384]{1,0:T(2,128)S(1)}, f32[2,384]{1,0:T(2,128)S(1)}, u32[]{:S(2)}, u32[]{:S(2)}) collective-permute-start(f32[2,384]{1,0:T(2,128)S(1)} %pad_maximum_fusion), channel_id=1, source_target_pairs={{0,12},{1,13},{2,14},{3,15},{4,0},{5,1},{6,2},{7,3},{8,4},{9,5},{1... | collective-permute-start | bytes 9224 | tf_op jit(solution)/shard_map/ppermute | solution.py:70
  164.5 4.0 %collective-permute-done.24 = f32[2,384]{1,0:T(2,128)S(1)} collective-permute-done((f32[2,384]{1,0:T(2,128)S(1)}, f32[2,384]{1,0:T(2,128)S(1)}, u32[]{:S(2)}, u32[]{:S(2)}) %collective-permute-start.24) | collective-permute-done | bytes 3104 | tf_op jit(solution)/shard_map/ppermute | solution.py:70
  (190 shorter events, 44.3 us)
Async XLA Ops:
  5.4 16.5 %all-to-all-start.1 = ((bf16[32,4,1024]{2,1,0:T(4,128)(2,1)}), bf16[32,4,1024]{2,1,0:T(4,128)(2,1)S(1)}, u32[]{:S(2)}, u32[]{:S(2)}) async-start(bf16[32,4,1024]{2,1,0:T(4,128)(2,1)} %reshape.252), calls=%async_computation.1 | async-start | bytes 524288 | tf_op jit(solution)/shard_map/all_to_all | solution.py:62
  22.0 12.7 %all-to-all-start = ((bf16[32,4,1024]{2,1,0:T(4,128)(2,1)}), bf16[32,4,1024]{2,1,0:T(4,128)(2,1)S(1)}, u32[]{:S(2)}, u32[]{:S(2)}) async-start(bf16[32,4,1024]{2,1,0:T(4,128)(2,1)} %reshape.250), calls=%async_computation | async-start | bytes 524288 | tf_op jit(solution)/shard_map/all_to_all | solution.py:62
  34.6 24.6 %all-to-all-start.2 = ((bf16[32,4,1024]{2,1,0:T(4,128)(2,1)}), bf16[32,4,1024]{2,1,0:T(4,128)(2,1)S(1)}, u32[]{:S(2)}, u32[]{:S(2)}) async-start(bf16[32,4,1024]{2,1,0:T(4,128)(2,1)} %reshape.254), calls=%async_computation.2 | async-start | bytes 524288 | tf_op jit(solution)/shard_map/all_to_all | solution.py:62
  40.6 26.1 %collective-permute-start.9 = (bf16[128,1024]{1,0:T(8,128)(2,1)S(1)}, bf16[128,1024]{1,0:T(8,128)(2,1)S(1)}, u32[]{:S(2)}, u32[]{:S(2)}) collective-permute-start(bf16[128,1024]{1,0:T(8,128)(2,1)S(1)} %reshape.251), channel_id=1, source_target_pairs={{0,1},{1,2},{2,3},{3,4},{4,5},{5,6},{6,7},{7,8},{8,9},{9,10},{10,1... | collective-permute-start | bytes 786440 | tf_op jit(solution)/shard_map/ppermute | solution.py:70
  42.5 21.0 %collective-permute-start = (bf16[128,1024]{1,0:T(8,128)(2,1)S(1)}, bf16[128,1024]{1,0:T(8,128)(2,1)S(1)}, u32[]{:S(2)}, u32[]{:S(2)}) collective-permute-start(bf16[128,1024]{1,0:T(8,128)(2,1)S(1)} %reshape.251), channel_id=1, source_target_pairs={{0,15},{1,0},{2,1},{3,2},{4,3},{5,4},{6,5},{7,6},{8,7},{9,8},{10,9... | collective-permute-start | bytes 786440 | tf_op jit(solution)/shard_map/ppermute | solution.py:70
  52.1 26.4 %collective-permute-start.11 = (bf16[128,1024]{1,0:T(8,128)(2,1)S(1)}, bf16[128,1024]{1,0:T(8,128)(2,1)S(1)}, u32[]{:S(2)}, u32[]{:S(2)}) collective-permute-start(bf16[128,1024]{1,0:T(8,128)(2,1)S(1)} %reshape.253), channel_id=1, source_target_pairs={{0,1},{1,2},{2,3},{3,4},{4,5},{5,6},{6,7},{7,8},{8,9},{9,10},{10,1... | collective-permute-start | bytes 786440 | tf_op jit(solution)/shard_map/ppermute | solution.py:70
  54.1 16.6 %collective-permute-start.1 = (bf16[128,1024]{1,0:T(8,128)(2,1)S(1)}, bf16[128,1024]{1,0:T(8,128)(2,1)S(1)}, u32[]{:S(2)}, u32[]{:S(2)}) collective-permute-start(bf16[128,1024]{1,0:T(8,128)(2,1)S(1)} %reshape.253), channel_id=1, source_target_pairs={{0,15},{1,0},{2,1},{3,2},{4,3},{5,4},{6,5},{7,6},{8,7},{9,8},{10,9... | collective-permute-start | bytes 786440 | tf_op jit(solution)/shard_map/ppermute | solution.py:70
  59.3 13.3 %collective-permute-start.2 = (bf16[128,1024]{1,0:T(8,128)(2,1)S(1)}, bf16[128,1024]{1,0:T(8,128)(2,1)S(1)}, u32[]{:S(2)}, u32[]{:S(2)}) collective-permute-start(bf16[128,1024]{1,0:T(8,128)(2,1)S(1)} %reshape.255), channel_id=1, source_target_pairs={{0,15},{1,0},{2,1},{3,2},{4,3},{5,4},{6,5},{7,6},{8,7},{9,8},{10,9... | collective-permute-start | bytes 786440 | tf_op jit(solution)/shard_map/ppermute | solution.py:70
  63.6 16.9 %collective-permute-start.13 = (bf16[128,1024]{1,0:T(8,128)(2,1)S(1)}, bf16[128,1024]{1,0:T(8,128)(2,1)S(1)}, u32[]{:S(2)}, u32[]{:S(2)}) collective-permute-start(bf16[128,1024]{1,0:T(8,128)(2,1)S(1)} %reshape.255), channel_id=1, source_target_pairs={{0,1},{1,2},{2,3},{3,4},{4,5},{5,6},{6,7},{7,8},{8,9},{9,10},{10,1... | collective-permute-start | bytes 786440 | tf_op jit(solution)/shard_map/ppermute | solution.py:70
  66.7 17.7 %collective-permute-start.3 = (bf16[128,1024]{1,0:T(8,128)(2,1)S(1)}, bf16[128,1024]{1,0:T(8,128)(2,1)S(1)}, u32[]{:S(2)}, u32[]{:S(2)}) collective-permute-start(bf16[128,1024]{1,0:T(8,128)(2,1)S(1)} %collective-permute-done), channel_id=1, source_target_pairs={{0,15},{1,0},{2,1},{3,2},{4,3},{5,4},{6,5},{7,6},{8,7},{9,8},{10,9... | collective-permute-start | bytes 786440 | tf_op jit(solution)/shard_map/ppermute | solution.py:70
  70.7 15.7 %collective-permute-start.10 = (bf16[128,1024]{1,0:T(8,128)(2,1)S(1)}, bf16[128,1024]{1,0:T(8,128)(2,1)S(1)}, u32[]{:S(2)}, u32[]{:S(2)}) collective-permute-start(bf16[128,1024]{1,0:T(8,128)(2,1)S(1)} %collective-permute-done.9), channel_id=1, source_target_pairs={{0,1},{1,2},{2,3},{3,4},{4,5},{5,6},{6,7},{7,8},{8,9},{9,10},{10,1... | collective-permute-start | bytes 786440 | tf_op jit(solution)/shard_map/ppermute | solution.py:70
  73.3 18.3 %collective-permute-start.4 = (bf16[128,1024]{1,0:T(8,128)(2,1)S(1)}, bf16[128,1024]{1,0:T(8,128)(2,1)S(1)}, u32[]{:S(2)}, u32[]{:S(2)}) collective-permute-start(bf16[128,1024]{1,0:T(8,128)(2,1)S(1)} %collective-permute-done.1), channel_id=1, source_target_pairs={{0,15},{1,0},{2,1},{3,2},{4,3},{5,4},{6,5},{7,6},{8,7},{9,8},{10,9... | collective-permute-start | bytes 786440 | tf_op jit(solution)/shard_map/ppermute | solution.py:70
  78.6 13.1 %collective-permute-start.5 = (bf16[128,1024]{1,0:T(8,128)(2,1)S(1)}, bf16[128,1024]{1,0:T(8,128)(2,1)S(1)}, u32[]{:S(2)}, u32[]{:S(2)}) collective-permute-start(bf16[128,1024]{1,0:T(8,128)(2,1)S(1)} %collective-permute-done.2), channel_id=1, source_target_pairs={{0,15},{1,0},{2,1},{3,2},{4,3},{5,4},{6,5},{7,6},{8,7},{9,8},{10,9... | collective-permute-start | bytes 786440 | tf_op jit(solution)/shard_map/ppermute | solution.py:70
  80.5 12.3 %collective-permute-start.12 = (bf16[128,1024]{1,0:T(8,128)(2,1)S(1)}, bf16[128,1024]{1,0:T(8,128)(2,1)S(1)}, u32[]{:S(2)}, u32[]{:S(2)}) collective-permute-start(bf16[128,1024]{1,0:T(8,128)(2,1)S(1)} %collective-permute-done.11), channel_id=1, source_target_pairs={{0,1},{1,2},{2,3},{3,4},{4,5},{5,6},{6,7},{7,8},{8,9},{9,10},{10,1... | collective-permute-start | bytes 786440 | tf_op jit(solution)/shard_map/ppermute | solution.py:70
  86.4 21.0 %collective-permute-start.6 = (bf16[128,1024]{1,0:T(8,128)(2,1)S(1)}, bf16[128,1024]{1,0:T(8,128)(2,1)S(1)}, u32[]{:S(2)}, u32[]{:S(2)}) collective-permute-start(bf16[128,1024]{1,0:T(8,128)(2,1)S(1)} %collective-permute-done.3), channel_id=1, source_target_pairs={{0,15},{1,0},{2,1},{3,2},{4,3},{5,4},{6,5},{7,6},{8,7},{9,8},{10,9... | collective-permute-start | bytes 786440 | tf_op jit(solution)/shard_map/ppermute | solution.py:70
  96.2 16.3 %collective-permute-start.15 = (bf16[128,1024]{1,0:T(8,128)(2,1)S(1)}, bf16[128,1024]{1,0:T(8,128)(2,1)S(1)}, u32[]{:S(2)}, u32[]{:S(2)}) collective-permute-start(bf16[128,1024]{1,0:T(8,128)(2,1)S(1)} %collective-permute-done.10), channel_id=1, source_target_pairs={{0,1},{1,2},{2,3},{3,4},{4,5},{5,6},{6,7},{7,8},{8,9},{9,10},{10,1... | collective-permute-start | bytes 786440 | tf_op jit(solution)/shard_map/ppermute | solution.py:70
  98.3 18.3 %collective-permute-start.7 = (bf16[128,1024]{1,0:T(8,128)(2,1)S(1)}, bf16[128,1024]{1,0:T(8,128)(2,1)S(1)}, u32[]{:S(2)}, u32[]{:S(2)}) collective-permute-start(bf16[128,1024]{1,0:T(8,128)(2,1)S(1)} %collective-permute-done.4), channel_id=1, source_target_pairs={{0,15},{1,0},{2,1},{3,2},{4,3},{5,4},{6,5},{7,6},{8,7},{9,8},{10,9... | collective-permute-start | bytes 786440 | tf_op jit(solution)/shard_map/ppermute | solution.py:70
  103.5 15.2 %collective-permute-start.16 = (bf16[128,1024]{1,0:T(8,128)(2,1)S(1)}, bf16[128,1024]{1,0:T(8,128)(2,1)S(1)}, u32[]{:S(2)}, u32[]{:S(2)}) collective-permute-start(bf16[128,1024]{1,0:T(8,128)(2,1)S(1)} %collective-permute-done.12), channel_id=1, source_target_pairs={{0,1},{1,2},{2,3},{3,4},{4,5},{5,6},{6,7},{7,8},{8,9},{9,10},{10,1... | collective-permute-start | bytes 786440 | tf_op jit(solution)/shard_map/ppermute | solution.py:70
  105.4 13.9 %collective-permute-start.17 = (bf16[128,1024]{1,0:T(8,128)(2,1)S(1)}, bf16[128,1024]{1,0:T(8,128)(2,1)S(1)}, u32[]{:S(2)}, u32[]{:S(2)}) collective-permute-start(bf16[128,1024]{1,0:T(8,128)(2,1)S(1)} %collective-permute-done.14), channel_id=1, source_target_pairs={{0,1},{1,2},{2,3},{3,4},{4,5},{5,6},{6,7},{7,8},{8,9},{9,10},{10,1... | collective-permute-start | bytes 786440 | tf_op jit(solution)/shard_map/ppermute | solution.py:70
  112.6 19.1 %collective-permute-start.21 = (bf16[128,1024]{1,0:T(8,128)(2,1)S(1)}, bf16[128,1024]{1,0:T(8,128)(2,1)S(1)}, u32[]{:S(2)}, u32[]{:S(2)}) collective-permute-start(bf16[128,1024]{1,0:T(8,128)(2,1)S(1)} %collective-permute-done.6), channel_id=1, source_target_pairs={{0,15},{1,0},{2,1},{3,2},{4,3},{5,4},{6,5},{7,6},{8,7},{9,8},{10,9... | collective-permute-start | bytes 786440 | tf_op jit(solution)/shard_map/ppermute | solution.py:70
  120.0 17.0 %collective-permute-start.18 = (bf16[128,1024]{1,0:T(8,128)(2,1)S(1)}, bf16[128,1024]{1,0:T(8,128)(2,1)S(1)}, u32[]{:S(2)}, u32[]{:S(2)}) collective-permute-start(bf16[128,1024]{1,0:T(8,128)(2,1)S(1)} %collective-permute-done.15), channel_id=1, source_target_pairs={{0,1},{1,2},{2,3},{3,4},{4,5},{5,6},{6,7},{7,8},{8,9},{9,10},{10,1... | collective-permute-start | bytes 786440 | tf_op jit(solution)/shard_map/ppermute | solution.py:70
  122.1 15.0 %collective-permute-start.22 = (bf16[128,1024]{1,0:T(8,128)(2,1)S(1)}, bf16[128,1024]{1,0:T(8,128)(2,1)S(1)}, u32[]{:S(2)}, u32[]{:S(2)}) collective-permute-start(bf16[128,1024]{1,0:T(8,128)(2,1)S(1)} %collective-permute-done.7), channel_id=1, source_target_pairs={{0,15},{1,0},{2,1},{3,2},{4,3},{5,4},{6,5},{7,6},{8,7},{9,8},{10,9... | collective-permute-start | bytes 786440 | tf_op jit(solution)/shard_map/ppermute | solution.py:70
  127.8 12.9 %collective-permute-start.19 = (bf16[128,1024]{1,0:T(8,128)(2,1)S(1)}, bf16[128,1024]{1,0:T(8,128)(2,1)S(1)}, u32[]{:S(2)}, u32[]{:S(2)}) collective-permute-start(bf16[128,1024]{1,0:T(8,128)(2,1)S(1)} %collective-permute-done.16), channel_id=1, source_target_pairs={{0,1},{1,2},{2,3},{3,4},{4,5},{5,6},{6,7},{7,8},{8,9},{9,10},{10,1... | collective-permute-start | bytes 786440 | tf_op jit(solution)/shard_map/ppermute | solution.py:70
  144.0 24.6 %all-to-all-start.3 = ((f32[16,3,384]{2,1,0:T(4,128)}), f32[16,3,384]{2,1,0:T(4,128)S(1)}, u32[]{:S(2)}, u32[]{:S(2)}) async-start(f32[16,3,384]{2,1,0:T(4,128)} %constant_dynamic-slice_fusion.1), calls=%async_computation.3 | async-start | bytes 196608 | tf_op jit(solution)/shard_map/all_to_all | solution.py:139
  (14 other events, 136.9 us)
where the time goes:
time: 171 us; the launch traced here: 169 us
  starting transfers between devices  125 us (73%)
  waiting for transfers between devices  23.1 us (14%)
  matrix products  7.52 us (4%)
  other arithmetic  7.32 us (4%)
  local copies, waits for them, and re-layouts  5.56 us (3%)
    ppermute x26, starting transfers between devices, shift(): lax.ppermute(value, 'grp', [(i, (i + offset) % grp_count) for i in range(...  95 us
    all_to_all x3, starting transfers between devices, per_device(): lax.all_to_all(h, 'wide', split_axis=0, concat_axis=0, tiled=True)  20.5 us
    ppermute x26, waiting for transfers between devices, shift(): lax.ppermute(value, 'grp', [(i, (i + offset) % grp_count) for i in range(...  12.5 us
    all_to_all x3, waiting for transfers between devices, per_device(): lax.all_to_all(h, 'wide', split_axis=0, concat_axis=0, tiled=True)  10.6 us
    all_to_all x1, starting transfers between devices, per_device(): lax.all_to_all(by_device, 'grp', split_axis=0, concat_axis=0, tiled=True)  9.46 us
    dot_general x9, matrix products, pair_products(): lax.dot_general(left_rows, right_rows, (((1,), (1,)), ((), ())), preferre...  6.03 us
  transfers between devices with their start and end apart: 30, of which 7 were waited for; matrix products, arithmetic and copies ran while one was open for 7% of the time, Pallas kernels for 0%

commit v1 on v0

--- a/solution.py
+++ b/solution.py
@@ -41,10 +41,9 @@
     row_ranks = jnp.sum(jnp.cumsum(onehot, axis=0) * onehot, axis=1) - 1
     send_slots = bucket * capacity + row_ranks
     sentinel_row = jnp.where(jnp.arange(feature_width) == 0, SENTINEL, 0.0).astype(jnp.float32)
-    parts = 3
-    split = capacity // parts
+    split = capacity // 2
     halves = []
-    for h in range(parts):
+    for h in range(2):
         slot_ids = (
             jnp.arange(wide_count, dtype=jnp.int32)[:, None] * capacity
             + h * split
@@ -148,12 +147,12 @@
         stacked = shift(jnp.stack([s for _, s in items]), target)
         slot_sums = slot_sums + weighted(stacked, items, target)
 
-    own_valid = valid_at[0].reshape(parts, wide_count, split).transpose(1, 0, 2).reshape(wide_count, capacity)
+    own_valid = valid_at[0].reshape(2, wide_count, split).transpose(1, 0, 2).reshape(wide_count, capacity)
     arrived = jnp.sum(own_valid, axis=1).astype(jnp.int32)
     offsets = jnp.cumsum(arrived) - arrived
     within = jnp.arange(capacity, dtype=jnp.int32)
     places = jnp.where(own_valid > 0, offsets[:, None] + within[None, :], BLK)
-    places = places.reshape(wide_count, parts, split).transpose(1, 0, 2).reshape(-1)
+    places = places.reshape(wide_count, 2, split).transpose(1, 0, 2).reshape(-1)
     rows_iota = jnp.arange(BLK, dtype=jnp.int32)
     density = jnp.sum(jnp.where(places[:, None] == rows_iota[None, :], slot_sums[:, None], 0.0), axis=0)
     return density.reshape(1, BLK)

time: 171 us -> 161 us (0.942)
  starting transfers between devices: 125 us -> 97.1 us
  waiting for transfers between devices: 23.1 us -> 42.5 us
    ppermute x26 -> x18, starting transfers between devices: 95 us -> 72.2 us  [shift(): lax.ppermute(value, 'grp', [(i, (i + offset) % grp_count) for i in range(...]
    ppermute x26 -> x18, waiting for transfers between devices: 12.5 us -> 35.2 us  [shift(): lax.ppermute(value, 'grp', [(i, (i + offset) % grp_count) for i in range(...]
    all_to_all x3 -> x2, starting transfers between devices: 20.5 us -> 15.5 us  [per_device(): lax.all_to_all(h, 'wide', split_axis=0, concat_axis=0, tiled=True)]
    all_to_all x3 -> x2, waiting for transfers between devices: 10.6 us -> 7.38 us  [per_device(): lax.all_to_all(h, 'wide', split_axis=0, concat_axis=0, tiled=True)]
  transfers between devices with their start and end apart: 30 -> 21, of which waited for: 7 -> 11; matrix products, arithmetic and copies ran while one was open for 7% -> 6% of each run, Pallas kernels for 0% -> 0%
where the time goes in v1:
time: 161 us; the launch traced here: 160 us
  starting transfers between devices  97.1 us (60%)
  waiting for transfers between devices  42.5 us (26%)
  other arithmetic  7.36 us (5%)
  matrix products  6.98 us (4%)
  local copies, waits for them, and re-layouts  5.12 us (3%)
    ppermute x18, starting transfers between devices, shift(): lax.ppermute(value, 'grp', [(i, (i + offset) % grp_count) for i in range(...  72.2 us
    ppermute x18, waiting for transfers between devices, shift(): lax.ppermute(value, 'grp', [(i, (i + offset) % grp_count) for i in range(...  35.2 us
    all_to_all x2, starting transfers between devices, per_device(): lax.all_to_all(h, 'wide', split_axis=0, concat_axis=0, tiled=True)  15.5 us
    all_to_all x1, starting transfers between devices, per_device(): lax.all_to_all(by_device, 'grp', split_axis=0, concat_axis=0, tiled=True)  9.41 us
    all_to_all x2, waiting for transfers between devices, per_device(): lax.all_to_all(h, 'wide', split_axis=0, concat_axis=0, tiled=True)  7.38 us
    dot_general x9, matrix products, pair_products(): lax.dot_general(left_rows, right_rows, (((1,), (1,)), ((), ())), preferre...  6.07 us
  transfers between devices with their start and end apart: 21, of which 11 were waited for; matrix products, arithmetic and copies ran while one was open for 6% of the time, Pallas kernels for 0%

profile of v1, /device:TPU:6, one launch (start us, length us, event | category | flops | bytes accessed | tf_op | source)
XLA Modules:
  0.0 159.8 jit_solution(13290947422540325893)
XLA Ops:
  5.4 9.4 %all-to-all-start = ((bf16[32,6,1024]{2,1,0:T(8,128)(2,1)}), bf16[32,6,1024]{2,1,0:T(8,128)(2,1)S(1)}, u32[]{:S(2)}, u32[]{:S(2)}) async-start(bf16[32,6,1024]{2,1,0:T(8,128)(2,1)} %reshape.226), calls=%async_computation | async-start | bytes 1048576 | tf_op jit(solution)/shard_map/all_to_all | solution.py:61
  16.8 7.4 %all-to-all-done = bf16[32,6,1024]{2,1,0:T(8,128)(2,1)S(1)} async-done(((bf16[32,6,1024]{2,1,0:T(8,128)(2,1)}), bf16[32,6,1024]{2,1,0:T(8,128)(2,1)S(1)}, u32[]{:S(2)}, u32[]{:S(2)}) %all-to-all-start) | async-done | bytes 393248 | tf_op jit(solution)/shard_map/all_to_all | solution.py:61
  24.2 6.1 %all-to-all-start.1 = ((bf16[32,6,1024]{2,1,0:T(8,128)(2,1)}), bf16[32,6,1024]{2,1,0:T(8,128)(2,1)S(1)}, u32[]{:S(2)}, u32[]{:S(2)}) async-start(bf16[32,6,1024]{2,1,0:T(8,128)(2,1)} %reshape.228), calls=%async_computation.1 | async-start | bytes 1048576 | tf_op jit(solution)/shard_map/all_to_all | solution.py:61
  31.3 1.9 %collective-permute-start.6 = (bf16[192,1024]{1,0:T(8,128)(2,1)S(1)}, bf16[192,1024]{1,0:T(8,128)(2,1)}, u32[]{:S(2)}, u32[]{:S(2)}) collective-permute-start(bf16[192,1024]{1,0:T(8,128)(2,1)S(1)} %reshape.227), channel_id=1, source_target_pairs={{0,1},{1,2},{2,3},{3,4},{4,5},{5,6},{6,7},{7,8},{8,9},{9,10},{10,1... | collective-permute-start | bytes 1179656 | tf_op jit(solution)/shard_map/ppermute | solution.py:69
  33.3 9.5 %collective-permute-start = (bf16[192,1024]{1,0:T(8,128)(2,1)S(1)}, bf16[192,1024]{1,0:T(8,128)(2,1)S(1)}, u32[]{:S(2)}, u32[]{:S(2)}) collective-permute-start(bf16[192,1024]{1,0:T(8,128)(2,1)S(1)} %reshape.227), channel_id=1, source_target_pairs={{0,15},{1,0},{2,1},{3,2},{4,3},{5,4},{6,5},{7,6},{8,7},{9,8},{10,9... | collective-permute-start | bytes 1179656 | tf_op jit(solution)/shard_map/ppermute | solution.py:69
  42.9 1.9 %collective-permute-start.8 = (bf16[192,1024]{1,0:T(8,128)(2,1)S(1)}, bf16[192,1024]{1,0:T(8,128)(2,1)}, u32[]{:S(2)}, u32[]{:S(2)}) collective-permute-start(bf16[192,1024]{1,0:T(8,128)(2,1)S(1)} %reshape.229), channel_id=1, source_target_pairs={{0,1},{1,2},{2,3},{3,4},{4,5},{5,6},{6,7},{7,8},{8,9},{9,10},{10,1... | collective-permute-start | bytes 1179656 | tf_op jit(solution)/shard_map/ppermute | solution.py:69
  44.8 6.4 %collective-permute-start.1 = (bf16[192,1024]{1,0:T(8,128)(2,1)S(1)}, bf16[192,1024]{1,0:T(8,128)(2,1)S(1)}, u32[]{:S(2)}, u32[]{:S(2)}) collective-permute-start(bf16[192,1024]{1,0:T(8,128)(2,1)S(1)} %reshape.229), channel_id=1, source_target_pairs={{0,15},{1,0},{2,1},{3,2},{4,3},{5,4},{6,5},{7,6},{8,7},{9,8},{10,9... | collective-permute-start | bytes 1179656 | tf_op jit(solution)/shard_map/ppermute | solution.py:69
  54.8 5.1 %collective-permute-start.2 = (bf16[192,1024]{1,0:T(8,128)(2,1)S(1)}, bf16[192,1024]{1,0:T(8,128)(2,1)S(1)}, u32[]{:S(2)}, u32[]{:S(2)}) collective-permute-start(bf16[192,1024]{1,0:T(8,128)(2,1)S(1)} %collective-permute-done), channel_id=1, source_target_pairs={{0,15},{1,0},{2,1},{3,2},{4,3},{5,4},{6,5},{7,6},{8,7},{9,8},{10,9... | collective-permute-start | bytes 1179656 | tf_op jit(solution)/shard_map/ppermute | solution.py:69
  60.7 5.6 %collective-permute-start.3 = (bf16[192,1024]{1,0:T(8,128)(2,1)S(1)}, bf16[192,1024]{1,0:T(8,128)(2,1)S(1)}, u32[]{:S(2)}, u32[]{:S(2)}) collective-permute-start(bf16[192,1024]{1,0:T(8,128)(2,1)S(1)} %collective-permute-done.1), channel_id=1, source_target_pairs={{0,15},{1,0},{2,1},{3,2},{4,3},{5,4},{6,5},{7,6},{8,7},{9,8},{10,9... | collective-permute-start | bytes 1179656 | tf_op jit(solution)/shard_map/ppermute | solution.py:69
  69.5 8.1 %collective-permute-done.3 = bf16[192,1024]{1,0:T(8,128)(2,1)S(1)} collective-permute-done((bf16[192,1024]{1,0:T(8,128)(2,1)S(1)}, bf16[192,1024]{1,0:T(8,128)(2,1)S(1)}, u32[]{:S(2)}, u32[]{:S(2)}) %collective-permute-start.3) | collective-permute-done | bytes 393248 | tf_op jit(solution)/shard_map/ppermute | solution.py:69
  77.8 3.4 %collective-permute-done.9 = bf16[192,1024]{1,0:T(8,128)(2,1)S(1)} collective-permute-done((bf16[192,1024]{1,0:T(8,128)(2,1)}, bf16[192,1024]{1,0:T(8,128)(2,1)S(1)}, u32[]{:S(2)}, u32[]{:S(2)}) %collective-permute-start.9) | collective-permute-done | bytes 393248 | tf_op jit(solution)/shard_map/ppermute | solution.py:69
  83.8 5.1 %collective-permute-start.4 = (bf16[192,1024]{1,0:T(8,128)(2,1)S(1)}, bf16[192,1024]{1,0:T(8,128)(2,1)S(1)}, u32[]{:S(2)}, u32[]{:S(2)}) collective-permute-start(bf16[192,1024]{1,0:T(8,128)(2,1)S(1)} %collective-permute-done.2), channel_id=1, source_target_pairs={{0,15},{1,0},{2,1},{3,2},{4,3},{5,4},{6,5},{7,6},{8,7},{9,8},{10,9... | collective-permute-start | bytes 1179656 | tf_op jit(solution)/shard_map/ppermute | solution.py:69
  90.9 5.1 %collective-permute-start.5 = (bf16[192,1024]{1,0:T(8,128)(2,1)S(1)}, bf16[192,1024]{1,0:T(8,128)(2,1)S(1)}, u32[]{:S(2)}, u32[]{:S(2)}) collective-permute-start(bf16[192,1024]{1,0:T(8,128)(2,1)S(1)} %collective-permute-done.3), channel_id=1, source_target_pairs={{0,15},{1,0},{2,1},{3,2},{4,3},{5,4},{6,5},{7,6},{8,7},{9,8},{10,9... | collective-permute-start | bytes 1179656 | tf_op jit(solution)/shard_map/ppermute | solution.py:69
  98.1 6.5 %collective-permute-done.5 = bf16[192,1024]{1,0:T(8,128)(2,1)S(1)} collective-permute-done((bf16[192,1024]{1,0:T(8,128)(2,1)S(1)}, bf16[192,1024]{1,0:T(8,128)(2,1)S(1)}, u32[]{:S(2)}, u32[]{:S(2)}) %collective-permute-start.5) | collective-permute-done | bytes 393248 | tf_op jit(solution)/shard_map/ppermute | solution.py:69
  105.3 1.9 %collective-permute-start.12 = (bf16[192,1024]{1,0:T(8,128)(2,1)S(1)}, bf16[192,1024]{1,0:T(8,128)(2,1)S(1)}, u32[]{:S(2)}, u32[]{:S(2)}) collective-permute-start(bf16[192,1024]{1,0:T(8,128)(2,1)S(1)} %collective-permute-done.10), channel_id=1, source_target_pairs={{0,1},{1,2},{2,3},{3,4},{4,5},{5,6},{6,7},{7,8},{8,9},{9,10},{10,1... | collective-permute-start | bytes 1179656 | tf_op jit(solution)/shard_map/ppermute | solution.py:69
  107.8 1.9 %collective-permute-start.13 = (bf16[192,1024]{1,0:T(8,128)(2,1)S(1)}, bf16[192,1024]{1,0:T(8,128)(2,1)S(1)}, u32[]{:S(2)}, u32[]{:S(2)}) collective-permute-start(bf16[192,1024]{1,0:T(8,128)(2,1)S(1)} %collective-permute-done.11), channel_id=1, source_target_pairs={{0,1},{1,2},{2,3},{3,4},{4,5},{5,6},{6,7},{7,8},{8,9},{9,10},{10,1... | collective-permute-start | bytes 1179656 | tf_op jit(solution)/shard_map/ppermute | solution.py:69
  110.4 5.6 %collective-permute-start.14 = (bf16[192,1024]{1,0:T(8,128)(2,1)S(1)}, bf16[192,1024]{1,0:T(8,128)(2,1)S(1)}, u32[]{:S(2)}, u32[]{:S(2)}) collective-permute-start(bf16[192,1024]{1,0:T(8,128)(2,1)S(1)} %collective-permute-done.4), channel_id=1, source_target_pairs={{0,15},{1,0},{2,1},{3,2},{4,3},{5,4},{6,5},{7,6},{8,7},{9,8},{10,9... | collective-permute-start | bytes 1179656 | tf_op jit(solution)/shard_map/ppermute | solution.py:69
  116.3 4.1 %collective-permute-start.15 = (bf16[192,1024]{1,0:T(8,128)(2,1)S(1)}, bf16[192,1024]{1,0:T(8,128)(2,1)S(1)}, u32[]{:S(2)}, u32[]{:S(2)}) collective-permute-start(bf16[192,1024]{1,0:T(8,128)(2,1)S(1)} %collective-permute-done.5), channel_id=1, source_target_pairs={{0,15},{1,0},{2,1},{3,2},{4,3},{5,4},{6,5},{7,6},{8,7},{9,8},{10,9... | collective-permute-start | bytes 1179656 | tf_op jit(solution)/shard_map/ppermute | solution.py:69
  120.9 5.9 %collective-permute-done.13 = bf16[192,1024]{1,0:T(8,128)(2,1)S(1)} collective-permute-done((bf16[192,1024]{1,0:T(8,128)(2,1)S(1)}, bf16[192,1024]{1,0:T(8,128)(2,1)S(1)}, u32[]{:S(2)}, u32[]{:S(2)}) %collective-permute-start.13) | collective-permute-done | bytes 393248 | tf_op jit(solution)/shard_map/ppermute | solution.py:69
  126.9 4.2 %collective-permute-done.15 = bf16[192,1024]{1,0:T(8,128)(2,1)S(1)} collective-permute-done((bf16[192,1024]{1,0:T(8,128)(2,1)S(1)}, bf16[192,1024]{1,0:T(8,128)(2,1)S(1)}, u32[]{:S(2)}, u32[]{:S(2)}) %collective-permute-start.15) | collective-permute-done | bytes 393248 | tf_op jit(solution)/shard_map/ppermute | solution.py:69
  134.3 9.4 %all-to-all-start.2 = ((f32[16,3,384]{2,1,0:T(4,128)}), f32[16,3,384]{2,1,0:T(4,128)S(1)}, u32[]{:S(2)}, u32[]{:S(2)}) async-start(f32[16,3,384]{2,1,0:T(4,128)} %constant_dynamic-slice_fusion.1), calls=%async_computation.2 | async-start | bytes 196608 | tf_op jit(solution)/shard_map/all_to_all | solution.py:138
  143.8 5.6 %collective-permute-start.17 = (f32[1,384]{1,0:T(1,128)S(1)}, f32[1,384]{1,0:T(1,128)S(1)}, u32[]{:S(2)}, u32[]{:S(2)}) collective-permute-start(f32[1,384]{1,0:T(1,128)S(1)} %stack.116), channel_id=1, source_target_pairs={{0,3},{1,4},{2,5},{3,6},{4,7},{5,8},{6,9},{7,10},{8,11},{9,12},{10... | collective-permute-start | bytes 4616 | tf_op jit(solution)/shard_map/ppermute | solution.py:69
  149.4 4.6 %collective-permute-start.16 = (f32[2,384]{1,0:T(2,128)S(1)}, f32[2,384]{1,0:T(2,128)S(1)}, u32[]{:S(2)}, u32[]{:S(2)}) collective-permute-start(f32[2,384]{1,0:T(2,128)S(1)} %pad_maximum_fusion), channel_id=1, source_target_pairs={{0,12},{1,13},{2,14},{3,15},{4,0},{5,1},{6,2},{7,3},{8,4},{9,5},{1... | collective-permute-start | bytes 9224 | tf_op jit(solution)/shard_map/ppermute | solution.py:69
  154.8 4.0 %collective-permute-done.16 = f32[2,384]{1,0:T(2,128)S(1)} collective-permute-done((f32[2,384]{1,0:T(2,128)S(1)}, f32[2,384]{1,0:T(2,128)S(1)}, u32[]{:S(2)}, u32[]{:S(2)}) %collective-permute-start.16) | collective-permute-done | bytes 3104 | tf_op jit(solution)/shard_map/ppermute | solution.py:69
  (158 shorter events, 30.1 us)
Async XLA Ops:
  4.5 10.4 %copy-start.6 = (s32[16]{0:T(128)S(1)}, s32[16]{0:T(128)}, u32[]{:S(2)}) copy-start(s32[16]{0:T(128)} %param.10) | copy-start | bytes 196
  5.4 18.8 %all-to-all-start = ((bf16[32,6,1024]{2,1,0:T(8,128)(2,1)}), bf16[32,6,1024]{2,1,0:T(8,128)(2,1)S(1)}, u32[]{:S(2)}, u32[]{:S(2)}) async-start(bf16[32,6,1024]{2,1,0:T(8,128)(2,1)} %reshape.226), calls=%async_computation | async-start | bytes 1048576 | tf_op jit(solution)/shard_map/all_to_all | solution.py:61
  15.6 14.8 %copy-start.7 = (f32[16]{0:T(128)S(1)}, f32[16]{0:T(128)}, u32[]{:S(2)}) copy-start(f32[16]{0:T(128)} %constant.102) | copy-start | bytes 196
  15.6 15.4 %copy-start.4 = (f32[4,16]{1,0:T(4,128)S(1)}, f32[4,16]{1,0:T(4,128)}, u32[]{:S(2)}) copy-start(f32[4,16]{1,0:T(4,128)} %constant.88.clone) | copy-start | bytes 772
  24.2 18.5 %all-to-all-start.1 = ((bf16[32,6,1024]{2,1,0:T(8,128)(2,1)}), bf16[32,6,1024]{2,1,0:T(8,128)(2,1)S(1)}, u32[]{:S(2)}, u32[]{:S(2)}) async-start(bf16[32,6,1024]{2,1,0:T(8,128)(2,1)} %reshape.228), calls=%async_computation.1 | async-start | bytes 1048576 | tf_op jit(solution)/shard_map/all_to_all | solution.py:61
  31.3 21.6 %collective-permute-start.6 = (bf16[192,1024]{1,0:T(8,128)(2,1)S(1)}, bf16[192,1024]{1,0:T(8,128)(2,1)}, u32[]{:S(2)}, u32[]{:S(2)}) collective-permute-start(bf16[192,1024]{1,0:T(8,128)(2,1)S(1)} %reshape.227), channel_id=1, source_target_pairs={{0,1},{1,2},{2,3},{3,4},{4,5},{5,6},{6,7},{7,8},{8,9},{9,10},{10,1... | collective-permute-start | bytes 1179656 | tf_op jit(solution)/shard_map/ppermute | solution.py:69
  33.3 21.6 %collective-permute-start = (bf16[192,1024]{1,0:T(8,128)(2,1)S(1)}, bf16[192,1024]{1,0:T(8,128)(2,1)S(1)}, u32[]{:S(2)}, u32[]{:S(2)}) collective-permute-start(bf16[192,1024]{1,0:T(8,128)(2,1)S(1)} %reshape.227), channel_id=1, source_target_pairs={{0,15},{1,0},{2,1},{3,2},{4,3},{5,4},{6,5},{7,6},{8,7},{9,8},{10,9... | collective-permute-start | bytes 1179656 | tf_op jit(solution)/shard_map/ppermute | solution.py:69
  42.9 24.2 %collective-permute-start.8 = (bf16[192,1024]{1,0:T(8,128)(2,1)S(1)}, bf16[192,1024]{1,0:T(8,128)(2,1)}, u32[]{:S(2)}, u32[]{:S(2)}) collective-permute-start(bf16[192,1024]{1,0:T(8,128)(2,1)S(1)} %reshape.229), channel_id=1, source_target_pairs={{0,1},{1,2},{2,3},{3,4},{4,5},{5,6},{6,7},{7,8},{8,9},{9,10},{10,1... | collective-permute-start | bytes 1179656 | tf_op jit(solution)/shard_map/ppermute | solution.py:69
  44.8 15.9 %collective-permute-start.1 = (bf16[192,1024]{1,0:T(8,128)(2,1)S(1)}, bf16[192,1024]{1,0:T(8,128)(2,1)S(1)}, u32[]{:S(2)}, u32[]{:S(2)}) collective-permute-start(bf16[192,1024]{1,0:T(8,128)(2,1)S(1)} %reshape.229), channel_id=1, source_target_pairs={{0,15},{1,0},{2,1},{3,2},{4,3},{5,4},{6,5},{7,6},{8,7},{9,8},{10,9... | collective-permute-start | bytes 1179656 | tf_op jit(solution)/shard_map/ppermute | solution.py:69
  52.9 24.9 %collective-permute-start.7 = (bf16[192,1024]{1,0:T(8,128)(2,1)}, bf16[192,1024]{1,0:T(8,128)(2,1)S(1)}, u32[]{:S(2)}, u32[]{:S(2)}) collective-permute-start(bf16[192,1024]{1,0:T(8,128)(2,1)} %collective-permute-done.6), channel_id=1, source_target_pairs={{0,1},{1,2},{2,3},{3,4},{4,5},{5,6},{6,7},{7,8},{8,9},{9,10},{10,1... | collective-permute-start | bytes 1179656 | tf_op jit(solution)/shard_map/ppermute | solution.py:69
  54.8 14.6 %collective-permute-start.2 = (bf16[192,1024]{1,0:T(8,128)(2,1)S(1)}, bf16[192,1024]{1,0:T(8,128)(2,1)S(1)}, u32[]{:S(2)}, u32[]{:S(2)}) collective-permute-start(bf16[192,1024]{1,0:T(8,128)(2,1)S(1)} %collective-permute-done), channel_id=1, source_target_pairs={{0,15},{1,0},{2,1},{3,2},{4,3},{5,4},{6,5},{7,6},{8,7},{9,8},{10,9... | collective-permute-start | bytes 1179656 | tf_op jit(solution)/shard_map/ppermute | solution.py:69
  60.7 16.9 %collective-permute-start.3 = (bf16[192,1024]{1,0:T(8,128)(2,1)S(1)}, bf16[192,1024]{1,0:T(8,128)(2,1)S(1)}, u32[]{:S(2)}, u32[]{:S(2)}) collective-permute-start(bf16[192,1024]{1,0:T(8,128)(2,1)S(1)} %collective-permute-done.1), channel_id=1, source_target_pairs={{0,15},{1,0},{2,1},{3,2},{4,3},{5,4},{6,5},{7,6},{8,7},{9,8},{10,9... | collective-permute-start | bytes 1179656 | tf_op jit(solution)/shard_map/ppermute | solution.py:69
  67.1 14.2 %collective-permute-start.9 = (bf16[192,1024]{1,0:T(8,128)(2,1)}, bf16[192,1024]{1,0:T(8,128)(2,1)S(1)}, u32[]{:S(2)}, u32[]{:S(2)}) collective-permute-start(bf16[192,1024]{1,0:T(8,128)(2,1)} %collective-permute-done.8), channel_id=1, source_target_pairs={{0,1},{1,2},{2,3},{3,4},{4,5},{5,6},{6,7},{7,8},{8,9},{9,10},{10,1... | collective-permute-start | bytes 1179656 | tf_op jit(solution)/shard_map/ppermute | solution.py:69
  81.9 23.4 %collective-permute-start.10 = (bf16[192,1024]{1,0:T(8,128)(2,1)S(1)}, bf16[192,1024]{1,0:T(8,128)(2,1)S(1)}, u32[]{:S(2)}, u32[]{:S(2)}) collective-permute-start(bf16[192,1024]{1,0:T(8,128)(2,1)S(1)} %collective-permute-done.7), channel_id=1, source_target_pairs={{0,1},{1,2},{2,3},{3,4},{4,5},{5,6},{6,7},{7,8},{8,9},{9,10},{10,1... | collective-permute-start | bytes 1179656 | tf_op jit(solution)/shard_map/ppermute | solution.py:69
  83.8 14.3 %collective-permute-start.4 = (bf16[192,1024]{1,0:T(8,128)(2,1)S(1)}, bf16[192,1024]{1,0:T(8,128)(2,1)S(1)}, u32[]{:S(2)}, u32[]{:S(2)}) collective-permute-start(bf16[192,1024]{1,0:T(8,128)(2,1)S(1)} %collective-permute-done.2), channel_id=1, source_target_pairs={{0,15},{1,0},{2,1},{3,2},{4,3},{5,4},{6,5},{7,6},{8,7},{9,8},{10,9... | collective-permute-start | bytes 1179656 | tf_op jit(solution)/shard_map/ppermute | solution.py:69
  89.0 18.9 %collective-permute-start.11 = (bf16[192,1024]{1,0:T(8,128)(2,1)S(1)}, bf16[192,1024]{1,0:T(8,128)(2,1)S(1)}, u32[]{:S(2)}, u32[]{:S(2)}) collective-permute-start(bf16[192,1024]{1,0:T(8,128)(2,1)S(1)} %collective-permute-done.9), channel_id=1, source_target_pairs={{0,1},{1,2},{2,3},{3,4},{4,5},{5,6},{6,7},{7,8},{8,9},{9,10},{10,1... | collective-permute-start | bytes 1179656 | tf_op jit(solution)/shard_map/ppermute | solution.py:69
  90.9 13.7 %collective-permute-start.5 = (bf16[192,1024]{1,0:T(8,128)(2,1)S(1)}, bf16[192,1024]{1,0:T(8,128)(2,1)S(1)}, u32[]{:S(2)}, u32[]{:S(2)}) collective-permute-start(bf16[192,1024]{1,0:T(8,128)(2,1)S(1)} %collective-permute-done.3), channel_id=1, source_target_pairs={{0,15},{1,0},{2,1},{3,2},{4,3},{5,4},{6,5},{7,6},{8,7},{9,8},{10,9... | collective-permute-start | bytes 1179656 | tf_op jit(solution)/shard_map/ppermute | solution.py:69
  105.3 15.6 %collective-permute-start.12 = (bf16[192,1024]{1,0:T(8,128)(2,1)S(1)}, bf16[192,1024]{1,0:T(8,128)(2,1)S(1)}, u32[]{:S(2)}, u32[]{:S(2)}) collective-permute-start(bf16[192,1024]{1,0:T(8,128)(2,1)S(1)} %collective-permute-done.10), channel_id=1, source_target_pairs={{0,1},{1,2},{2,3},{3,4},{4,5},{5,6},{6,7},{7,8},{8,9},{9,10},{10,1... | collective-permute-start | bytes 1179656 | tf_op jit(solution)/shard_map/ppermute | solution.py:69
  107.8 18.9 %collective-permute-start.13 = (bf16[192,1024]{1,0:T(8,128)(2,1)S(1)}, bf16[192,1024]{1,0:T(8,128)(2,1)S(1)}, u32[]{:S(2)}, u32[]{:S(2)}) collective-permute-start(bf16[192,1024]{1,0:T(8,128)(2,1)S(1)} %collective-permute-done.11), channel_id=1, source_target_pairs={{0,1},{1,2},{2,3},{3,4},{4,5},{5,6},{6,7},{7,8},{8,9},{9,10},{10,1... | collective-permute-start | bytes 1179656 | tf_op jit(solution)/shard_map/ppermute | solution.py:69
  110.4 16.5 %collective-permute-start.14 = (bf16[192,1024]{1,0:T(8,128)(2,1)S(1)}, bf16[192,1024]{1,0:T(8,128)(2,1)S(1)}, u32[]{:S(2)}, u32[]{:S(2)}) collective-permute-start(bf16[192,1024]{1,0:T(8,128)(2,1)S(1)} %collective-permute-done.4), channel_id=1, source_target_pairs={{0,15},{1,0},{2,1},{3,2},{4,3},{5,4},{6,5},{7,6},{8,7},{9,8},{10,9... | collective-permute-start | bytes 1179656 | tf_op jit(solution)/shard_map/ppermute | solution.py:69
  116.3 14.9 %collective-permute-start.15 = (bf16[192,1024]{1,0:T(8,128)(2,1)S(1)}, bf16[192,1024]{1,0:T(8,128)(2,1)S(1)}, u32[]{:S(2)}, u32[]{:S(2)}) collective-permute-start(bf16[192,1024]{1,0:T(8,128)(2,1)S(1)} %collective-permute-done.5), channel_id=1, source_target_pairs={{0,15},{1,0},{2,1},{3,2},{4,3},{5,4},{6,5},{7,6},{8,7},{9,8},{10,9... | collective-permute-start | bytes 1179656 | tf_op jit(solution)/shard_map/ppermute | solution.py:69
  134.3 24.6 %all-to-all-start.2 = ((f32[16,3,384]{2,1,0:T(4,128)}), f32[16,3,384]{2,1,0:T(4,128)S(1)}, u32[]{:S(2)}, u32[]{:S(2)}) async-start(f32[16,3,384]{2,1,0:T(4,128)} %constant_dynamic-slice_fusion.1), calls=%async_computation.2 | async-start | bytes 196608 | tf_op jit(solution)/shard_map/all_to_all | solution.py:138
  143.8 10.3 %collective-permute-start.17 = (f32[1,384]{1,0:T(1,128)S(1)}, f32[1,384]{1,0:T(1,128)S(1)}, u32[]{:S(2)}, u32[]{:S(2)}) collective-permute-start(f32[1,384]{1,0:T(1,128)S(1)} %stack.116), channel_id=1, source_target_pairs={{0,3},{1,4},{2,5},{3,6},{4,7},{5,8},{6,9},{7,10},{8,11},{9,12},{10... | collective-permute-start | bytes 4616 | tf_op jit(solution)/shard_map/ppermute | solution.py:69
  149.4 9.4 %collective-permute-start.16 = (f32[2,384]{1,0:T(2,128)S(1)}, f32[2,384]{1,0:T(2,128)S(1)}, u32[]{:S(2)}, u32[]{:S(2)}) collective-permute-start(f32[2,384]{1,0:T(2,128)S(1)} %pad_maximum_fusion), channel_id=1, source_target_pairs={{0,12},{1,13},{2,14},{3,15},{4,0},{5,1},{6,2},{7,3},{8,4},{9,5},{1... | collective-permute-start | bytes 9224 | tf_op jit(solution)/shard_map/ppermute | solution.py:69
  (5 other events, 10.6 us)

commit v2 on v1

--- a/solution.py
+++ b/solution.py
@@ -70,7 +70,8 @@
             value, "grp", [(i, (i + offset) % grp_count) for i in range(grp_count)]
         )
 
-    reach = 4
+    reach = 5
+    reach_right = 3
     rows_at = {}
     for part in own_halves:
         left = part
@@ -78,9 +79,10 @@
         rows_at.setdefault(0, []).append(part)
         for step in range(1, reach + 1):
             left = shift(left, 1)
-            right = shift(right, -1)
             rows_at.setdefault(-step, []).append(left)
-            rows_at.setdefault(step, []).append(right)
+            if step <= reach_right:
+                right = shift(right, -1)
+                rows_at.setdefault(step, []).append(right)
     halves_at = rows_at
     rows_at = {}
     valid_at = {}
@@ -102,11 +104,10 @@
         e = pair_products(rows_at[p], rows_at[q])
         to_p = jnp.sum(e * valid_at[q][None, :], axis=1)
         to_q = jnp.sum(e * valid_at[p][:, None], axis=0)
-        group = late if max(-p, q) == reach else early
-        add(group, p, q, to_p)
-        add(group, q, p, to_q)
-    e = pair_products(rows_at[-reach], rows_at[reach])
-    add(late, -reach, reach, jnp.sum(e * valid_at[reach][None, :], axis=1))
+        add(early, p, q, to_p)
+        add(early, q, p, to_q)
+    e = pair_products(rows_at[-reach], rows_at[reach_right])
+    add(late, -reach, reach_right, jnp.sum(e * valid_at[reach_right][None, :], axis=1))
 
     def near_at(offsets):
         hits = (np.asarray(offsets)[..., None] % grp_count) == np.arange(grp_count)

time: 161 us -> 162 us (level)
  starting transfers between devices: 97.1 us -> 83.7 us
  waiting for transfers between devices: 42.5 us -> 55.6 us
    ppermute x18 -> x17, starting transfers between devices: 72.2 us -> 59.2 us  [shift(): lax.ppermute(value, 'grp', [(i, (i + offset) % grp_count) for i in range(...]
    ppermute x18 -> x17, waiting for transfers between devices: 35.2 us -> 48 us  [shift(): lax.ppermute(value, 'grp', [(i, (i + offset) % grp_count) for i in range(...]
  transfers between devices with their start and end apart: 21 -> 20, of which waited for: 11 -> 12; matrix products, arithmetic and copies ran while one was open for 6% -> 7% of each run, Pallas kernels for 0% -> 0%
where the time goes in v2:
time: 162 us; the launch traced here: 160 us
  starting transfers between devices  83.7 us (52%)
  waiting for transfers between devices  55.6 us (34%)
  matrix products  7.97 us (5%)
  other arithmetic  7.5 us (5%)
  local copies, waits for them, and re-layouts  4.99 us (3%)
    ppermute x17, starting transfers between devices, shift(): lax.ppermute(value, 'grp', [(i, (i + offset) % grp_count) for i in range(...  59.2 us
    ppermute x17, waiting for transfers between devices, shift(): lax.ppermute(value, 'grp', [(i, (i + offset) % grp_count) for i in range(...  48 us
    all_to_all x2, starting transfers between devices, per_device(): lax.all_to_all(h, 'wide', split_axis=0, concat_axis=0, tiled=True)  15.5 us
    all_to_all x1, starting transfers between devices, per_device(): lax.all_to_all(by_device, 'grp', split_axis=0, concat_axis=0, tiled=True)  9 us
    all_to_all x2, waiting for transfers between devices, per_device(): lax.all_to_all(h, 'wide', split_axis=0, concat_axis=0, tiled=True)  7.6 us
    dot_general x9, matrix products, pair_products(): lax.dot_general(left_rows, right_rows, (((1,), (1,)), ((), ())), preferre...  7.05 us
  transfers between devices with their start and end apart: 20, of which 12 were waited for; matrix products, arithmetic and copies ran while one was open for 7% of the time, Pallas kernels for 0%

profile of v2, /device:TPU:6, one launch (start us, length us, event | category | flops | bytes accessed | tf_op | source)
XLA Modules:
  0.0 160.4 jit_solution(3334235561333052854)
XLA Ops:
  5.4 9.4 %all-to-all-start = ((bf16[32,6,1024]{2,1,0:T(8,128)(2,1)}), bf16[32,6,1024]{2,1,0:T(8,128)(2,1)S(1)}, u32[]{:S(2)}, u32[]{:S(2)}) async-start(bf16[32,6,1024]{2,1,0:T(8,128)(2,1)} %reshape.210), calls=%async_computation | async-start | bytes 1048576 | tf_op jit(solution)/shard_map/all_to_all | solution.py:61
  16.6 7.6 %all-to-all-done = bf16[32,6,1024]{2,1,0:T(8,128)(2,1)S(1)} async-done(((bf16[32,6,1024]{2,1,0:T(8,128)(2,1)}), bf16[32,6,1024]{2,1,0:T(8,128)(2,1)S(1)}, u32[]{:S(2)}, u32[]{:S(2)}) %all-to-all-start) | async-done | bytes 393248 | tf_op jit(solution)/shard_map/all_to_all | solution.py:61
  24.2 6.1 %all-to-all-start.1 = ((bf16[32,6,1024]{2,1,0:T(8,128)(2,1)}), bf16[32,6,1024]{2,1,0:T(8,128)(2,1)S(1)}, u32[]{:S(2)}, u32[]{:S(2)}) async-start(bf16[32,6,1024]{2,1,0:T(8,128)(2,1)} %reshape.212), calls=%async_computation.1 | async-start | bytes 1048576 | tf_op jit(solution)/shard_map/all_to_all | solution.py:61
  31.4 1.9 %collective-permute-start.6 = (bf16[192,1024]{1,0:T(8,128)(2,1)S(1)}, bf16[192,1024]{1,0:T(8,128)(2,1)}, u32[]{:S(2)}, u32[]{:S(2)}) collective-permute-start(bf16[192,1024]{1,0:T(8,128)(2,1)S(1)} %reshape.211), channel_id=1, source_target_pairs={{0,1},{1,2},{2,3},{3,4},{4,5},{5,6},{6,7},{7,8},{8,9},{9,10},{10,1... | collective-permute-start | bytes 1179656 | tf_op jit(solution)/shard_map/ppermute | solution.py:69
  33.3 9.5 %collective-permute-start = (bf16[192,1024]{1,0:T(8,128)(2,1)S(1)}, bf16[192,1024]{1,0:T(8,128)(2,1)S(1)}, u32[]{:S(2)}, u32[]{:S(2)}) collective-permute-start(bf16[192,1024]{1,0:T(8,128)(2,1)S(1)} %reshape.211), channel_id=1, source_target_pairs={{0,15},{1,0},{2,1},{3,2},{4,3},{5,4},{6,5},{7,6},{8,7},{9,8},{10,9... | collective-permute-start | bytes 1179656 | tf_op jit(solution)/shard_map/ppermute | solution.py:69
  43.0 1.9 %collective-permute-start.8 = (bf16[192,1024]{1,0:T(8,128)(2,1)S(1)}, bf16[192,1024]{1,0:T(8,128)(2,1)S(1)}, u32[]{:S(2)}, u32[]{:S(2)}) collective-permute-start(bf16[192,1024]{1,0:T(8,128)(2,1)S(1)} %reshape.213), channel_id=1, source_target_pairs={{0,1},{1,2},{2,3},{3,4},{4,5},{5,6},{6,7},{7,8},{8,9},{9,10},{10,1... | collective-permute-start | bytes 1179656 | tf_op jit(solution)/shard_map/ppermute | solution.py:69
  44.9 6.4 %collective-permute-start.1 = (bf16[192,1024]{1,0:T(8,128)(2,1)S(1)}, bf16[192,1024]{1,0:T(8,128)(2,1)S(1)}, u32[]{:S(2)}, u32[]{:S(2)}) collective-permute-start(bf16[192,1024]{1,0:T(8,128)(2,1)S(1)} %reshape.213), channel_id=1, source_target_pairs={{0,15},{1,0},{2,1},{3,2},{4,3},{5,4},{6,5},{7,6},{8,7},{9,8},{10,9... | collective-permute-start | bytes 1179656 | tf_op jit(solution)/shard_map/ppermute | solution.py:69
  54.2 5.1 %collective-permute-start.2 = (bf16[192,1024]{1,0:T(8,128)(2,1)S(1)}, bf16[192,1024]{1,0:T(8,128)(2,1)S(1)}, u32[]{:S(2)}, u32[]{:S(2)}) collective-permute-start(bf16[192,1024]{1,0:T(8,128)(2,1)S(1)} %collective-permute-done), channel_id=1, source_target_pairs={{0,15},{1,0},{2,1},{3,2},{4,3},{5,4},{6,5},{7,6},{8,7},{9,8},{10,9... | collective-permute-start | bytes 1179656 | tf_op jit(solution)/shard_map/ppermute | solution.py:69
  60.7 5.6 %collective-permute-start.3 = (bf16[192,1024]{1,0:T(8,128)(2,1)S(1)}, bf16[192,1024]{1,0:T(8,128)(2,1)S(1)}, u32[]{:S(2)}, u32[]{:S(2)}) collective-permute-start(bf16[192,1024]{1,0:T(8,128)(2,1)S(1)} %collective-permute-done.1), channel_id=1, source_target_pairs={{0,15},{1,0},{2,1},{3,2},{4,3},{5,4},{6,5},{7,6},{8,7},{9,8},{10,9... | collective-permute-start | bytes 1179656 | tf_op jit(solution)/shard_map/ppermute | solution.py:69
  67.0 1.9 %collective-permute-start.9 = (bf16[192,1024]{1,0:T(8,128)(2,1)S(1)}, bf16[192,1024]{1,0:T(8,128)(2,1)S(1)}, u32[]{:S(2)}, u32[]{:S(2)}) collective-permute-start(bf16[192,1024]{1,0:T(8,128)(2,1)S(1)} %collective-permute-done.8), channel_id=1, source_target_pairs={{0,1},{1,2},{2,3},{3,4},{4,5},{5,6},{6,7},{7,8},{8,9},{9,10},{10,1... | collective-permute-start | bytes 1179656 | tf_op jit(solution)/shard_map/ppermute | solution.py:69
  69.0 1.9 %collective-permute-start.10 = (bf16[192,1024]{1,0:T(8,128)(2,1)S(1)}, bf16[192,1024]{1,0:T(8,128)(2,1)S(1)}, u32[]{:S(2)}, u32[]{:S(2)}) collective-permute-start(bf16[192,1024]{1,0:T(8,128)(2,1)S(1)} %collective-permute-done.7), channel_id=1, source_target_pairs={{0,1},{1,2},{2,3},{3,4},{4,5},{5,6},{6,7},{7,8},{8,9},{9,10},{10,1... | collective-permute-start | bytes 1179656 | tf_op jit(solution)/shard_map/ppermute | solution.py:69
  71.0 5.1 %collective-permute-start.4 = (bf16[192,1024]{1,0:T(8,128)(2,1)S(1)}, bf16[192,1024]{1,0:T(8,128)(2,1)S(1)}, u32[]{:S(2)}, u32[]{:S(2)}) collective-permute-start(bf16[192,1024]{1,0:T(8,128)(2,1)S(1)} %collective-permute-done.2), channel_id=1, source_target_pairs={{0,15},{1,0},{2,1},{3,2},{4,3},{5,4},{6,5},{7,6},{8,7},{9,8},{10,9... | collective-permute-start | bytes 1179656 | tf_op jit(solution)/shard_map/ppermute | solution.py:69
  78.2 3.8 %collective-permute-done.9 = bf16[192,1024]{1,0:T(8,128)(2,1)S(1)} collective-permute-done((bf16[192,1024]{1,0:T(8,128)(2,1)S(1)}, bf16[192,1024]{1,0:T(8,128)(2,1)S(1)}, u32[]{:S(2)}, u32[]{:S(2)}) %collective-permute-start.9) | collective-permute-done | bytes 393248 | tf_op jit(solution)/shard_map/ppermute | solution.py:69
  82.7 1.9 %collective-permute-start.5 = (bf16[192,1024]{1,0:T(8,128)(2,1)S(1)}, bf16[192,1024]{1,0:T(8,128)(2,1)S(1)}, u32[]{:S(2)}, u32[]{:S(2)}) collective-permute-start(bf16[192,1024]{1,0:T(8,128)(2,1)S(1)} %collective-permute-done.3), channel_id=1, source_target_pairs={{0,15},{1,0},{2,1},{3,2},{4,3},{5,4},{6,5},{7,6},{8,7},{9,8},{10,9... | collective-permute-start | bytes 1179656 | tf_op jit(solution)/shard_map/ppermute | solution.py:69
  84.7 3.9 %collective-permute-start.11 = (bf16[192,1024]{1,0:T(8,128)(2,1)S(1)}, bf16[192,1024]{1,0:T(8,128)(2,1)S(1)}, u32[]{:S(2)}, u32[]{:S(2)}) collective-permute-start(bf16[192,1024]{1,0:T(8,128)(2,1)S(1)} %collective-permute-done.9), channel_id=1, source_target_pairs={{0,1},{1,2},{2,3},{3,4},{4,5},{5,6},{6,7},{7,8},{8,9},{9,10},{10,1... | collective-permute-start | bytes 1179656 | tf_op jit(solution)/shard_map/ppermute | solution.py:69
  89.5 4.9 %collective-permute-done.5 = bf16[192,1024]{1,0:T(8,128)(2,1)S(1)} collective-permute-done((bf16[192,1024]{1,0:T(8,128)(2,1)S(1)}, bf16[192,1024]{1,0:T(8,128)(2,1)S(1)}, u32[]{:S(2)}, u32[]{:S(2)}) %collective-permute-start.5) | collective-permute-done | bytes 393248 | tf_op jit(solution)/shard_map/ppermute | solution.py:69
  95.2 3.5 %collective-permute-done.11 = bf16[192,1024]{1,0:T(8,128)(2,1)S(1)} collective-permute-done((bf16[192,1024]{1,0:T(8,128)(2,1)S(1)}, bf16[192,1024]{1,0:T(8,128)(2,1)S(1)}, u32[]{:S(2)}, u32[]{:S(2)}) %collective-permute-start.11) | collective-permute-done | bytes 393248 | tf_op jit(solution)/shard_map/ppermute | solution.py:69
  103.9 10.5 %collective-permute-done.12 = bf16[192,1024]{1,0:T(8,128)(2,1)S(1)} collective-permute-done((bf16[192,1024]{1,0:T(8,128)(2,1)S(1)}, bf16[192,1024]{1,0:T(8,128)(2,1)S(1)}, u32[]{:S(2)}, u32[]{:S(2)}) %collective-permute-start.12) | collective-permute-done | bytes 393248 | tf_op jit(solution)/shard_map/ppermute | solution.py:69
  114.4 6.4 %collective-permute-done.13 = bf16[192,1024]{1,0:T(8,128)(2,1)S(1)} collective-permute-done((bf16[192,1024]{1,0:T(8,128)(2,1)S(1)}, bf16[192,1024]{1,0:T(8,128)(2,1)S(1)}, u32[]{:S(2)}, u32[]{:S(2)}) %collective-permute-start.13) | collective-permute-done | bytes 393248 | tf_op jit(solution)/shard_map/ppermute | solution.py:69
  125.0 1.9 %collective-permute-start.15 = (bf16[192,1024]{1,0:T(8,128)(2,1)S(1)}, bf16[192,1024]{1,0:T(8,128)(2,1)}, u32[]{:S(2)}, u32[]{:S(2)}) collective-permute-start(bf16[192,1024]{1,0:T(8,128)(2,1)S(1)} %collective-permute-done.13), channel_id=1, source_target_pairs={{0,1},{1,2},{2,3},{3,4},{4,5},{5,6},{6,7},{7,8},{8,9},{9,10},{10,1... | collective-permute-start | bytes 1179656 | tf_op jit(solution)/shard_map/ppermute | solution.py:69
  127.6 9.0 %all-to-all-start.2 = ((f32[16,4,384]{2,1,0:T(4,128)}), f32[16,4,384]{2,1,0:T(4,128)S(1)}, u32[]{:S(2)}, u32[]{:S(2)}) async-start(f32[16,4,384]{2,1,0:T(4,128)} %constant_dynamic-slice_fusion.1), calls=%async_computation.2 | async-start | bytes 196608 | tf_op jit(solution)/shard_map/all_to_all | solution.py:139
  138.2 8.9 %collective-permute-done.15 = bf16[192,1024]{1,0:T(8,128)(2,1)} collective-permute-done((bf16[192,1024]{1,0:T(8,128)(2,1)S(1)}, bf16[192,1024]{1,0:T(8,128)(2,1)}, u32[]{:S(2)}, u32[]{:S(2)}) %collective-permute-start.15) | collective-permute-done | bytes 393248 | tf_op jit(solution)/shard_map/ppermute | solution.py:69
  148.7 4.4 %collective-permute-start.16 = (f32[1,384]{1,0:T(1,128)S(1)}, f32[1,384]{1,0:T(1,128)S(1)}, u32[]{:S(2)}, u32[]{:S(2)}) collective-permute-start(f32[1,384]{1,0:T(1,128)S(1)} %stack.120), channel_id=1, source_target_pairs={{0,11},{1,12},{2,13},{3,14},{4,15},{5,0},{6,1},{7,2},{8,3},{9,4},{... | collective-permute-start | bytes 4616 | tf_op jit(solution)/shard_map/ppermute | solution.py:69
  153.2 5.8 %collective-permute-done.16 = f32[1,384]{1,0:T(1,128)S(1)} collective-permute-done((f32[1,384]{1,0:T(1,128)S(1)}, f32[1,384]{1,0:T(1,128)S(1)}, u32[]{:S(2)}, u32[]{:S(2)}) %collective-permute-start.16) | collective-permute-done | bytes 1568 | tf_op jit(solution)/shard_map/ppermute | solution.py:69
  (150 shorter events, 32.3 us)
Async XLA Ops:
  0.0 4.0 %copy-start = (bf16[288,1024]{1,0:T(8,128)(2,1)S(1)}, bf16[288,1024]{1,0:T(8,128)(2,1)}, u32[]{:S(2)}) copy-start(bf16[288,1024]{1,0:T(8,128)(2,1)} %param.7) | copy-start | bytes 1769476
  4.5 10.4 %copy-start.5 = (s32[16]{0:T(128)S(1)}, s32[16]{0:T(128)}, u32[]{:S(2)}) copy-start(s32[16]{0:T(128)} %param.9) | copy-start | bytes 196
  5.4 18.8 %all-to-all-start = ((bf16[32,6,1024]{2,1,0:T(8,128)(2,1)}), bf16[32,6,1024]{2,1,0:T(8,128)(2,1)S(1)}, u32[]{:S(2)}, u32[]{:S(2)}) async-start(bf16[32,6,1024]{2,1,0:T(8,128)(2,1)} %reshape.210), calls=%async_computation | async-start | bytes 1048576 | tf_op jit(solution)/shard_map/all_to_all | solution.py:61
  16.4 14.2 %copy-start.6 = (f32[16]{0:T(128)S(1)}, f32[16]{0:T(128)}, u32[]{:S(2)}) copy-start(f32[16]{0:T(128)} %constant.95) | copy-start | bytes 196
  16.4 14.8 %copy-start.4 = (f32[4,16]{1,0:T(4,128)S(1)}, f32[4,16]{1,0:T(4,128)}, u32[]{:S(2)}) copy-start(f32[4,16]{1,0:T(4,128)} %constant.86.clone) | copy-start | bytes 772
  24.2 18.6 %all-to-all-start.1 = ((bf16[32,6,1024]{2,1,0:T(8,128)(2,1)}), bf16[32,6,1024]{2,1,0:T(8,128)(2,1)S(1)}, u32[]{:S(2)}, u32[]{:S(2)}) async-start(bf16[32,6,1024]{2,1,0:T(8,128)(2,1)} %reshape.212), calls=%async_computation.1 | async-start | bytes 1048576 | tf_op jit(solution)/shard_map/all_to_all | solution.py:61
  31.4 20.8 %collective-permute-start.6 = (bf16[192,1024]{1,0:T(8,128)(2,1)S(1)}, bf16[192,1024]{1,0:T(8,128)(2,1)}, u32[]{:S(2)}, u32[]{:S(2)}) collective-permute-start(bf16[192,1024]{1,0:T(8,128)(2,1)S(1)} %reshape.211), channel_id=1, source_target_pairs={{0,1},{1,2},{2,3},{3,4},{4,5},{5,6},{6,7},{7,8},{8,9},{9,10},{10,1... | collective-permute-start | bytes 1179656 | tf_op jit(solution)/shard_map/ppermute | solution.py:69
  33.3 20.9 %collective-permute-start = (bf16[192,1024]{1,0:T(8,128)(2,1)S(1)}, bf16[192,1024]{1,0:T(8,128)(2,1)S(1)}, u32[]{:S(2)}, u32[]{:S(2)}) collective-permute-start(bf16[192,1024]{1,0:T(8,128)(2,1)S(1)} %reshape.211), channel_id=1, source_target_pairs={{0,15},{1,0},{2,1},{3,2},{4,3},{5,4},{6,5},{7,6},{8,7},{9,8},{10,9... | collective-permute-start | bytes 1179656 | tf_op jit(solution)/shard_map/ppermute | solution.py:69
  43.0 24.0 %collective-permute-start.8 = (bf16[192,1024]{1,0:T(8,128)(2,1)S(1)}, bf16[192,1024]{1,0:T(8,128)(2,1)S(1)}, u32[]{:S(2)}, u32[]{:S(2)}) collective-permute-start(bf16[192,1024]{1,0:T(8,128)(2,1)S(1)} %reshape.213), channel_id=1, source_target_pairs={{0,1},{1,2},{2,3},{3,4},{4,5},{5,6},{6,7},{7,8},{8,9},{9,10},{10,1... | collective-permute-start | bytes 1179656 | tf_op jit(solution)/shard_map/ppermute | solution.py:69
  44.9 15.8 %collective-permute-start.1 = (bf16[192,1024]{1,0:T(8,128)(2,1)S(1)}, bf16[192,1024]{1,0:T(8,128)(2,1)S(1)}, u32[]{:S(2)}, u32[]{:S(2)}) collective-permute-start(bf16[192,1024]{1,0:T(8,128)(2,1)S(1)} %reshape.213), channel_id=1, source_target_pairs={{0,15},{1,0},{2,1},{3,2},{4,3},{5,4},{6,5},{7,6},{8,7},{9,8},{10,9... | collective-permute-start | bytes 1179656 | tf_op jit(solution)/shard_map/ppermute | solution.py:69
  52.3 16.8 %collective-permute-start.7 = (bf16[192,1024]{1,0:T(8,128)(2,1)}, bf16[192,1024]{1,0:T(8,128)(2,1)S(1)}, u32[]{:S(2)}, u32[]{:S(2)}) collective-permute-start(bf16[192,1024]{1,0:T(8,128)(2,1)} %collective-permute-done.6), channel_id=1, source_target_pairs={{0,1},{1,2},{2,3},{3,4},{4,5},{5,6},{6,7},{7,8},{8,9},{9,10},{10,1... | collective-permute-start | bytes 1179656 | tf_op jit(solution)/shard_map/ppermute | solution.py:69
  54.2 16.8 %collective-permute-start.2 = (bf16[192,1024]{1,0:T(8,128)(2,1)S(1)}, bf16[192,1024]{1,0:T(8,128)(2,1)S(1)}, u32[]{:S(2)}, u32[]{:S(2)}) collective-permute-start(bf16[192,1024]{1,0:T(8,128)(2,1)S(1)} %collective-permute-done), channel_id=1, source_target_pairs={{0,15},{1,0},{2,1},{3,2},{4,3},{5,4},{6,5},{7,6},{8,7},{9,8},{10,9... | collective-permute-start | bytes 1179656 | tf_op jit(solution)/shard_map/ppermute | solution.py:69
  60.7 16.9 %collective-permute-start.3 = (bf16[192,1024]{1,0:T(8,128)(2,1)S(1)}, bf16[192,1024]{1,0:T(8,128)(2,1)S(1)}, u32[]{:S(2)}, u32[]{:S(2)}) collective-permute-start(bf16[192,1024]{1,0:T(8,128)(2,1)S(1)} %collective-permute-done.1), channel_id=1, source_target_pairs={{0,15},{1,0},{2,1},{3,2},{4,3},{5,4},{6,5},{7,6},{8,7},{9,8},{10,9... | collective-permute-start | bytes 1179656 | tf_op jit(solution)/shard_map/ppermute | solution.py:69
  67.0 15.1 %collective-permute-start.9 = (bf16[192,1024]{1,0:T(8,128)(2,1)S(1)}, bf16[192,1024]{1,0:T(8,128)(2,1)S(1)}, u32[]{:S(2)}, u32[]{:S(2)}) collective-permute-start(bf16[192,1024]{1,0:T(8,128)(2,1)S(1)} %collective-permute-done.8), channel_id=1, source_target_pairs={{0,1},{1,2},{2,3},{3,4},{4,5},{5,6},{6,7},{7,8},{8,9},{9,10},{10,1... | collective-permute-start | bytes 1179656 | tf_op jit(solution)/shard_map/ppermute | solution.py:69
  69.0 20.5 %collective-permute-start.10 = (bf16[192,1024]{1,0:T(8,128)(2,1)S(1)}, bf16[192,1024]{1,0:T(8,128)(2,1)S(1)}, u32[]{:S(2)}, u32[]{:S(2)}) collective-permute-start(bf16[192,1024]{1,0:T(8,128)(2,1)S(1)} %collective-permute-done.7), channel_id=1, source_target_pairs={{0,1},{1,2},{2,3},{3,4},{4,5},{5,6},{6,7},{7,8},{8,9},{9,10},{10,1... | collective-permute-start | bytes 1179656 | tf_op jit(solution)/shard_map/ppermute | solution.py:69
  71.0 17.8 %collective-permute-start.4 = (bf16[192,1024]{1,0:T(8,128)(2,1)S(1)}, bf16[192,1024]{1,0:T(8,128)(2,1)S(1)}, u32[]{:S(2)}, u32[]{:S(2)}) collective-permute-start(bf16[192,1024]{1,0:T(8,128)(2,1)S(1)} %collective-permute-done.2), channel_id=1, source_target_pairs={{0,15},{1,0},{2,1},{3,2},{4,3},{5,4},{6,5},{7,6},{8,7},{9,8},{10,9... | collective-permute-start | bytes 1179656 | tf_op jit(solution)/shard_map/ppermute | solution.py:69
  82.7 11.7 %collective-permute-start.5 = (bf16[192,1024]{1,0:T(8,128)(2,1)S(1)}, bf16[192,1024]{1,0:T(8,128)(2,1)S(1)}, u32[]{:S(2)}, u32[]{:S(2)}) collective-permute-start(bf16[192,1024]{1,0:T(8,128)(2,1)S(1)} %collective-permute-done.3), channel_id=1, source_target_pairs={{0,15},{1,0},{2,1},{3,2},{4,3},{5,4},{6,5},{7,6},{8,7},{9,8},{10,9... | collective-permute-start | bytes 1179656 | tf_op jit(solution)/shard_map/ppermute | solution.py:69
  84.7 13.9 %collective-permute-start.11 = (bf16[192,1024]{1,0:T(8,128)(2,1)S(1)}, bf16[192,1024]{1,0:T(8,128)(2,1)S(1)}, u32[]{:S(2)}, u32[]{:S(2)}) collective-permute-start(bf16[192,1024]{1,0:T(8,128)(2,1)S(1)} %collective-permute-done.9), channel_id=1, source_target_pairs={{0,1},{1,2},{2,3},{3,4},{4,5},{5,6},{6,7},{7,8},{8,9},{9,10},{10,1... | collective-permute-start | bytes 1179656 | tf_op jit(solution)/shard_map/ppermute | solution.py:69
  99.3 15.1 %collective-permute-start.12 = (bf16[192,1024]{1,0:T(8,128)(2,1)S(1)}, bf16[192,1024]{1,0:T(8,128)(2,1)S(1)}, u32[]{:S(2)}, u32[]{:S(2)}) collective-permute-start(bf16[192,1024]{1,0:T(8,128)(2,1)S(1)} %collective-permute-done.10), channel_id=1, source_target_pairs={{0,1},{1,2},{2,3},{3,4},{4,5},{5,6},{6,7},{7,8},{8,9},{9,10},{10,1... | collective-permute-start | bytes 1179656 | tf_op jit(solution)/shard_map/ppermute | solution.py:69
  101.2 19.6 %collective-permute-start.13 = (bf16[192,1024]{1,0:T(8,128)(2,1)S(1)}, bf16[192,1024]{1,0:T(8,128)(2,1)S(1)}, u32[]{:S(2)}, u32[]{:S(2)}) collective-permute-start(bf16[192,1024]{1,0:T(8,128)(2,1)S(1)} %collective-permute-done.11), channel_id=1, source_target_pairs={{0,1},{1,2},{2,3},{3,4},{4,5},{5,6},{6,7},{7,8},{8,9},{9,10},{10,1... | collective-permute-start | bytes 1179656 | tf_op jit(solution)/shard_map/ppermute | solution.py:69
  123.1 15.1 %collective-permute-start.14 = (bf16[192,1024]{1,0:T(8,128)(2,1)S(1)}, bf16[192,1024]{1,0:T(8,128)(2,1)S(1)}, u32[]{:S(2)}, u32[]{:S(2)}) collective-permute-start(bf16[192,1024]{1,0:T(8,128)(2,1)S(1)} %collective-permute-done.12), channel_id=1, source_target_pairs={{0,1},{1,2},{2,3},{3,4},{4,5},{5,6},{6,7},{7,8},{8,9},{9,10},{10,1... | collective-permute-start | bytes 1179656 | tf_op jit(solution)/shard_map/ppermute | solution.py:69
  125.0 22.0 %collective-permute-start.15 = (bf16[192,1024]{1,0:T(8,128)(2,1)S(1)}, bf16[192,1024]{1,0:T(8,128)(2,1)}, u32[]{:S(2)}, u32[]{:S(2)}) collective-permute-start(bf16[192,1024]{1,0:T(8,128)(2,1)S(1)} %collective-permute-done.13), channel_id=1, source_target_pairs={{0,1},{1,2},{2,3},{3,4},{4,5},{5,6},{6,7},{7,8},{8,9},{9,10},{10,1... | collective-permute-start | bytes 1179656 | tf_op jit(solution)/shard_map/ppermute | solution.py:69
  127.6 25.5 %all-to-all-start.2 = ((f32[16,4,384]{2,1,0:T(4,128)}), f32[16,4,384]{2,1,0:T(4,128)S(1)}, u32[]{:S(2)}, u32[]{:S(2)}) async-start(f32[16,4,384]{2,1,0:T(4,128)} %constant_dynamic-slice_fusion.1), calls=%async_computation.2 | async-start | bytes 196608 | tf_op jit(solution)/shard_map/all_to_all | solution.py:139
  148.7 10.3 %collective-permute-start.16 = (f32[1,384]{1,0:T(1,128)S(1)}, f32[1,384]{1,0:T(1,128)S(1)}, u32[]{:S(2)}, u32[]{:S(2)}) collective-permute-start(f32[1,384]{1,0:T(1,128)S(1)} %stack.120), channel_id=1, source_target_pairs={{0,11},{1,12},{2,13},{3,14},{4,15},{5,0},{6,1},{7,2},{8,3},{9,4},{... | collective-permute-start | bytes 4616 | tf_op jit(solution)/shard_map/ppermute | solution.py:69
  (3 other events, 5.9 us)

commit v3 on v1

--- a/solution.py
+++ b/solution.py
@@ -1,6 +1,5 @@
 import jax
 import jax.numpy as jnp
-import numpy as np
 from jax import lax
 from jax.sharding import PartitionSpec as P
 
@@ -108,12 +107,8 @@
     e = pair_products(rows_at[-reach], rows_at[reach])
     add(late, -reach, reach, jnp.sum(e * valid_at[reach][None, :], axis=1))
 
-    def near_at(offsets):
-        hits = (np.asarray(offsets)[..., None] % grp_count) == np.arange(grp_count)
-        return jnp.sum(jnp.asarray(hits, jnp.float32) * near, axis=-1)
-
     def weighted(stacked, items, target):
-        weights = near_at([s - target for s, _ in items])
+        weights = jnp.stack([near[(s - target) % grp_count] for s, _ in items])
         return jnp.sum(stacked * weights[:, None], axis=0)
 
     slot_sums = weighted(jnp.stack([s for _, s in early[0]]), early[0], 0)
@@ -136,10 +131,13 @@
         jnp.concatenate([by_offset, by_offset], axis=0), start, grp_count, 0
     )
     arrived_sums = lax.all_to_all(by_device, "grp", split_axis=0, concat_axis=0, tiled=True)
-    gap_order = [(-g) % grp_count for g in range(grp_count)]
-    by_gap = near_at(np.asarray(source_table)[gap_order]) * jnp.asarray(
-        np.asarray(present_table, np.float32)[gap_order]
-    )
+    by_gap = jnp.stack([
+        jnp.stack([
+            near[source_table[(-g) % grp_count][k] % grp_count] * present_table[(-g) % grp_count][k]
+            for k in range(depth)
+        ])
+        for g in range(grp_count)
+    ])
     weights = lax.dynamic_slice_in_dim(jnp.concatenate([by_gap, by_gap], axis=0), start, grp_count, 0)
     slot_sums = slot_sums + jnp.sum(arrived_sums * weights[:, :, None], axis=(0, 1))
 

time: 161 us -> 162 us (level)
  waiting for transfers between devices: 42.5 us -> 37.1 us
  other arithmetic: 7.36 us -> 10.9 us
    all_to_all x2, waiting for transfers between devices: 7.38 us -> 2.02 us  [per_device(): lax.all_to_all(h, 'wide', split_axis=0, concat_axis=0, tiled=True)]
    another operation x6 -> x9, other arithmetic: 1.17 us -> 5.69 us  [the longest x3 4.52 us: per_device(): jnp.stack([jnp.stack([near[source_table[-g % grp_count][k] % grp_count] *...]
  transfers between devices with their start and end apart: 21 -> 21, of which waited for: 11 -> 11; matrix products, arithmetic and copies ran while one was open for 6% -> 9% of each run, Pallas kernels for 0% -> 0%
where the time goes in v3:
time: 162 us; the launch traced here: 160 us
  starting transfers between devices  97 us (60%)
  waiting for transfers between devices  37.1 us (23%)
  other arithmetic  10.9 us (7%)
  matrix products  6.98 us (4%)
  local copies, waits for them, and re-layouts  6.34 us (4%)
    ppermute x18, starting transfers between devices, shift(): lax.ppermute(value, 'grp', [(i, (i + offset) % grp_count) for i in range(...  72.2 us
    ppermute x18, waiting for transfers between devices, shift(): lax.ppermute(value, 'grp', [(i, (i + offset) % grp_count) for i in range(...  35.1 us
    all_to_all x2, starting transfers between devices, per_device(): lax.all_to_all(h, 'wide', split_axis=0, concat_axis=0, tiled=True)  15.5 us
    all_to_all x1, starting transfers between devices, per_device(): lax.all_to_all(by_device, 'grp', split_axis=0, concat_axis=0, tiled=True)  9.41 us
    dot_general x9, matrix products, pair_products(): lax.dot_general(left_rows, right_rows, (((1,), (1,)), ((), ())), preferre...  6.07 us
    another operation x3, other arithmetic, per_device(): jnp.stack([jnp.stack([near[source_table[-g % grp_count][k] % grp_count] *...  4.52 us
  transfers between devices with their start and end apart: 21, of which 11 were waited for; matrix products, arithmetic and copies ran while one was open for 9% of the time, Pallas kernels for 0%

profile of v3, /device:TPU:6, one launch (start us, length us, event | category | flops | bytes accessed | tf_op | source)
XLA Modules:
  0.0 159.7 jit_solution(9037653955674926907)
XLA Ops:
  5.4 9.4 %all-to-all-start = ((bf16[32,6,1024]{2,1,0:T(8,128)(2,1)}), bf16[32,6,1024]{2,1,0:T(8,128)(2,1)S(1)}, u32[]{:S(2)}, u32[]{:S(2)}) async-start(bf16[32,6,1024]{2,1,0:T(8,128)(2,1)} %reshape.223), calls=%async_computation | async-start | bytes 1048576 | tf_op jit(solution)/shard_map/all_to_all | solution.py:60
  16.7 2.0 %maximum_bitcast_fusion.6 = (f32[1,3]{1,0:T(1,128)S(1)}, f32[1,3]{1,0:T(1,128)S(1)}) fusion(f32[1]{0:T(128)} %get-tuple-element.37, f32[1]{0:T(128)} %get-tuple-element.38, f32[1]{0:T(128)} %mul.309, f32[1]{0:T(128)} %get-tuple-element.35), kind=kLoop, calls=%fused_computation.151 | loop fusion | flops 12 | bytes 40 | tf_op jit(solution)/shard_map/stack | solution.py:134
  19.6 2.5 %maximum_bitcast_fusion.4 = (f32[1,3]{1,0:T(1,128)S(1)}, f32[1,3]{1,0:T(1,128)S(1)}) fusion(f32[1]{0:T(128)} %get-tuple-element.42, f32[1]{0:T(128)} %mul.309, f32[1]{0:T(128)} %get-tuple-element.39, f32[1]{0:T(128)} %get-tuple-element.40, f32[1]{0:T(128)} %get-tuple-element.41), kind=kLoop, calls=%fused_computation.149 | loop fusion | flops 12 | bytes 44 | tf_op jit(solution)/shard_map/stack | solution.py:134
  22.2 2.0 %all-to-all-done = bf16[32,6,1024]{2,1,0:T(8,128)(2,1)S(1)} async-done(((bf16[32,6,1024]{2,1,0:T(8,128)(2,1)}), bf16[32,6,1024]{2,1,0:T(8,128)(2,1)S(1)}, u32[]{:S(2)}, u32[]{:S(2)}) %all-to-all-start) | async-done | bytes 393248 | tf_op jit(solution)/shard_map/all_to_all | solution.py:60
  24.2 6.1 %all-to-all-start.1 = ((bf16[32,6,1024]{2,1,0:T(8,128)(2,1)}), bf16[32,6,1024]{2,1,0:T(8,128)(2,1)S(1)}, u32[]{:S(2)}, u32[]{:S(2)}) async-start(bf16[32,6,1024]{2,1,0:T(8,128)(2,1)} %reshape.225), calls=%async_computation.1 | async-start | bytes 1048576 | tf_op jit(solution)/shard_map/all_to_all | solution.py:60
  31.3 1.9 %collective-permute-start.6 = (bf16[192,1024]{1,0:T(8,128)(2,1)S(1)}, bf16[192,1024]{1,0:T(8,128)(2,1)}, u32[]{:S(2)}, u32[]{:S(2)}) collective-permute-start(bf16[192,1024]{1,0:T(8,128)(2,1)S(1)} %reshape.224), channel_id=1, source_target_pairs={{0,1},{1,2},{2,3},{3,4},{4,5},{5,6},{6,7},{7,8},{8,9},{9,10},{10,1... | collective-permute-start | bytes 1179656 | tf_op jit(solution)/shard_map/ppermute | solution.py:68
  33.3 9.5 %collective-permute-start = (bf16[192,1024]{1,0:T(8,128)(2,1)S(1)}, bf16[192,1024]{1,0:T(8,128)(2,1)S(1)}, u32[]{:S(2)}, u32[]{:S(2)}) collective-permute-start(bf16[192,1024]{1,0:T(8,128)(2,1)S(1)} %reshape.224), channel_id=1, source_target_pairs={{0,15},{1,0},{2,1},{3,2},{4,3},{5,4},{6,5},{7,6},{8,7},{9,8},{10,9... | collective-permute-start | bytes 1179656 | tf_op jit(solution)/shard_map/ppermute | solution.py:68
  42.9 1.9 %collective-permute-start.8 = (bf16[192,1024]{1,0:T(8,128)(2,1)S(1)}, bf16[192,1024]{1,0:T(8,128)(2,1)}, u32[]{:S(2)}, u32[]{:S(2)}) collective-permute-start(bf16[192,1024]{1,0:T(8,128)(2,1)S(1)} %reshape.226), channel_id=1, source_target_pairs={{0,1},{1,2},{2,3},{3,4},{4,5},{5,6},{6,7},{7,8},{8,9},{9,10},{10,1... | collective-permute-start | bytes 1179656 | tf_op jit(solution)/shard_map/ppermute | solution.py:68
  44.8 6.4 %collective-permute-start.1 = (bf16[192,1024]{1,0:T(8,128)(2,1)S(1)}, bf16[192,1024]{1,0:T(8,128)(2,1)S(1)}, u32[]{:S(2)}, u32[]{:S(2)}) collective-permute-start(bf16[192,1024]{1,0:T(8,128)(2,1)S(1)} %reshape.226), channel_id=1, source_target_pairs={{0,15},{1,0},{2,1},{3,2},{4,3},{5,4},{6,5},{7,6},{8,7},{9,8},{10,9... | collective-permute-start | bytes 1179656 | tf_op jit(solution)/shard_map/ppermute | solution.py:68
  54.8 5.1 %collective-permute-start.2 = (bf16[192,1024]{1,0:T(8,128)(2,1)S(1)}, bf16[192,1024]{1,0:T(8,128)(2,1)S(1)}, u32[]{:S(2)}, u32[]{:S(2)}) collective-permute-start(bf16[192,1024]{1,0:T(8,128)(2,1)S(1)} %collective-permute-done), channel_id=1, source_target_pairs={{0,15},{1,0},{2,1},{3,2},{4,3},{5,4},{6,5},{7,6},{8,7},{9,8},{10,9... | collective-permute-start | bytes 1179656 | tf_op jit(solution)/shard_map/ppermute | solution.py:68
  60.7 5.6 %collective-permute-start.3 = (bf16[192,1024]{1,0:T(8,128)(2,1)S(1)}, bf16[192,1024]{1,0:T(8,128)(2,1)S(1)}, u32[]{:S(2)}, u32[]{:S(2)}) collective-permute-start(bf16[192,1024]{1,0:T(8,128)(2,1)S(1)} %collective-permute-done.1), channel_id=1, source_target_pairs={{0,15},{1,0},{2,1},{3,2},{4,3},{5,4},{6,5},{7,6},{8,7},{9,8},{10,9... | collective-permute-start | bytes 1179656 | tf_op jit(solution)/shard_map/ppermute | solution.py:68
  69.5 8.1 %collective-permute-done.3 = bf16[192,1024]{1,0:T(8,128)(2,1)S(1)} collective-permute-done((bf16[192,1024]{1,0:T(8,128)(2,1)S(1)}, bf16[192,1024]{1,0:T(8,128)(2,1)S(1)}, u32[]{:S(2)}, u32[]{:S(2)}) %collective-permute-start.3) | collective-permute-done | bytes 393248 | tf_op jit(solution)/shard_map/ppermute | solution.py:68
  77.8 3.4 %collective-permute-done.9 = bf16[192,1024]{1,0:T(8,128)(2,1)S(1)} collective-permute-done((bf16[192,1024]{1,0:T(8,128)(2,1)}, bf16[192,1024]{1,0:T(8,128)(2,1)S(1)}, u32[]{:S(2)}, u32[]{:S(2)}) %collective-permute-start.9) | collective-permute-done | bytes 393248 | tf_op jit(solution)/shard_map/ppermute | solution.py:68
  83.8 5.1 %collective-permute-start.4 = (bf16[192,1024]{1,0:T(8,128)(2,1)S(1)}, bf16[192,1024]{1,0:T(8,128)(2,1)S(1)}, u32[]{:S(2)}, u32[]{:S(2)}) collective-permute-start(bf16[192,1024]{1,0:T(8,128)(2,1)S(1)} %collective-permute-done.2), channel_id=1, source_target_pairs={{0,15},{1,0},{2,1},{3,2},{4,3},{5,4},{6,5},{7,6},{8,7},{9,8},{10,9... | collective-permute-start | bytes 1179656 | tf_op jit(solution)/shard_map/ppermute | solution.py:68
  90.9 5.1 %collective-permute-start.5 = (bf16[192,1024]{1,0:T(8,128)(2,1)S(1)}, bf16[192,1024]{1,0:T(8,128)(2,1)S(1)}, u32[]{:S(2)}, u32[]{:S(2)}) collective-permute-start(bf16[192,1024]{1,0:T(8,128)(2,1)S(1)} %collective-permute-done.3), channel_id=1, source_target_pairs={{0,15},{1,0},{2,1},{3,2},{4,3},{5,4},{6,5},{7,6},{8,7},{9,8},{10,9... | collective-permute-start | bytes 1179656 | tf_op jit(solution)/shard_map/ppermute | solution.py:68
  98.1 6.5 %collective-permute-done.5 = bf16[192,1024]{1,0:T(8,128)(2,1)S(1)} collective-permute-done((bf16[192,1024]{1,0:T(8,128)(2,1)S(1)}, bf16[192,1024]{1,0:T(8,128)(2,1)S(1)}, u32[]{:S(2)}, u32[]{:S(2)}) %collective-permute-start.5) | collective-permute-done | bytes 393248 | tf_op jit(solution)/shard_map/ppermute | solution.py:68
  110.4 5.6 %collective-permute-start.14 = (bf16[192,1024]{1,0:T(8,128)(2,1)S(1)}, bf16[192,1024]{1,0:T(8,128)(2,1)S(1)}, u32[]{:S(2)}, u32[]{:S(2)}) collective-permute-start(bf16[192,1024]{1,0:T(8,128)(2,1)S(1)} %collective-permute-done.4), channel_id=1, source_target_pairs={{0,15},{1,0},{2,1},{3,2},{4,3},{5,4},{6,5},{7,6},{8,7},{9,8},{10,9... | collective-permute-start | bytes 1179656 | tf_op jit(solution)/shard_map/ppermute | solution.py:68
  116.2 4.1 %collective-permute-start.15 = (bf16[192,1024]{1,0:T(8,128)(2,1)S(1)}, bf16[192,1024]{1,0:T(8,128)(2,1)S(1)}, u32[]{:S(2)}, u32[]{:S(2)}) collective-permute-start(bf16[192,1024]{1,0:T(8,128)(2,1)S(1)} %collective-permute-done.5), channel_id=1, source_target_pairs={{0,15},{1,0},{2,1},{3,2},{4,3},{5,4},{6,5},{7,6},{8,7},{9,8},{10,9... | collective-permute-start | bytes 1179656 | tf_op jit(solution)/shard_map/ppermute | solution.py:68
  120.8 5.9 %collective-permute-done.13 = bf16[192,1024]{1,0:T(8,128)(2,1)S(1)} collective-permute-done((bf16[192,1024]{1,0:T(8,128)(2,1)S(1)}, bf16[192,1024]{1,0:T(8,128)(2,1)S(1)}, u32[]{:S(2)}, u32[]{:S(2)}) %collective-permute-start.13) | collective-permute-done | bytes 393248 | tf_op jit(solution)/shard_map/ppermute | solution.py:68
  126.9 4.2 %collective-permute-done.15 = bf16[192,1024]{1,0:T(8,128)(2,1)S(1)} collective-permute-done((bf16[192,1024]{1,0:T(8,128)(2,1)S(1)}, bf16[192,1024]{1,0:T(8,128)(2,1)S(1)}, u32[]{:S(2)}, u32[]{:S(2)}) %collective-permute-start.15) | collective-permute-done | bytes 393248 | tf_op jit(solution)/shard_map/ppermute | solution.py:68
  134.3 9.4 %all-to-all-start.2 = ((f32[16,3,384]{2,1,0:T(4,128)}), f32[16,3,384]{2,1,0:T(4,128)S(1)}, u32[]{:S(2)}, u32[]{:S(2)}) async-start(f32[16,3,384]{2,1,0:T(4,128)} %constant_dynamic-slice_fusion.1), calls=%async_computation.2 | async-start | bytes 196608 | tf_op jit(solution)/shard_map/all_to_all | solution.py:133
  143.7 5.6 %collective-permute-start.17 = (f32[1,384]{1,0:T(1,128)S(1)}, f32[1,384]{1,0:T(1,128)S(1)}, u32[]{:S(2)}, u32[]{:S(2)}) collective-permute-start(f32[1,384]{1,0:T(1,128)S(1)} %stack.228), channel_id=1, source_target_pairs={{0,3},{1,4},{2,5},{3,6},{4,7},{5,8},{6,9},{7,10},{8,11},{9,12},{10... | collective-permute-start | bytes 4616 | tf_op jit(solution)/shard_map/ppermute | solution.py:68
  149.4 4.6 %collective-permute-start.16 = (f32[2,384]{1,0:T(2,128)S(1)}, f32[2,384]{1,0:T(2,128)S(1)}, u32[]{:S(2)}, u32[]{:S(2)}) collective-permute-start(f32[2,384]{1,0:T(2,128)S(1)} %pad_maximum_fusion), channel_id=1, source_target_pairs={{0,12},{1,13},{2,14},{3,15},{4,0},{5,1},{6,2},{7,3},{8,4},{9,5},{1... | collective-permute-start | bytes 9224 | tf_op jit(solution)/shard_map/ppermute | solution.py:68
  154.8 4.0 %collective-permute-done.16 = f32[2,384]{1,0:T(2,128)S(1)} collective-permute-done((f32[2,384]{1,0:T(2,128)S(1)}, f32[2,384]{1,0:T(2,128)S(1)}, u32[]{:S(2)}, u32[]{:S(2)}) %collective-permute-start.16) | collective-permute-done | bytes 3104 | tf_op jit(solution)/shard_map/ppermute | solution.py:68
  (154 shorter events, 34.3 us)
Async XLA Ops:
  0.0 4.0 %copy-start = (bf16[288,1024]{1,0:T(8,128)(2,1)S(1)}, bf16[288,1024]{1,0:T(8,128)(2,1)}, u32[]{:S(2)}) copy-start(bf16[288,1024]{1,0:T(8,128)(2,1)} %param.3) | copy-start | bytes 1769476
  0.0 3.7 %copy-start.1 = (s32[288]{0:T(512)S(1)}, s32[288]{0:T(512)}, u32[]{:S(2)}) copy-start(s32[288]{0:T(512)} %param.4) | copy-start | bytes 3460
  4.5 10.3 %copy-start.2 = (s32[16]{0:T(128)S(1)}, s32[16]{0:T(128)}, u32[]{:S(2)}) copy-start(s32[16]{0:T(128)} %param.5) | copy-start | bytes 196
  5.4 18.8 %all-to-all-start = ((bf16[32,6,1024]{2,1,0:T(8,128)(2,1)}), bf16[32,6,1024]{2,1,0:T(8,128)(2,1)S(1)}, u32[]{:S(2)}, u32[]{:S(2)}) async-start(bf16[32,6,1024]{2,1,0:T(8,128)(2,1)} %reshape.223), calls=%async_computation | async-start | bytes 1048576 | tf_op jit(solution)/shard_map/all_to_all | solution.py:60
  24.2 18.6 %all-to-all-start.1 = ((bf16[32,6,1024]{2,1,0:T(8,128)(2,1)}), bf16[32,6,1024]{2,1,0:T(8,128)(2,1)S(1)}, u32[]{:S(2)}, u32[]{:S(2)}) async-start(bf16[32,6,1024]{2,1,0:T(8,128)(2,1)} %reshape.225), calls=%async_computation.1 | async-start | bytes 1048576 | tf_op jit(solution)/shard_map/all_to_all | solution.py:60
  31.3 21.5 %collective-permute-start.6 = (bf16[192,1024]{1,0:T(8,128)(2,1)S(1)}, bf16[192,1024]{1,0:T(8,128)(2,1)}, u32[]{:S(2)}, u32[]{:S(2)}) collective-permute-start(bf16[192,1024]{1,0:T(8,128)(2,1)S(1)} %reshape.224), channel_id=1, source_target_pairs={{0,1},{1,2},{2,3},{3,4},{4,5},{5,6},{6,7},{7,8},{8,9},{9,10},{10,1... | collective-permute-start | bytes 1179656 | tf_op jit(solution)/shard_map/ppermute | solution.py:68
  33.3 21.5 %collective-permute-start = (bf16[192,1024]{1,0:T(8,128)(2,1)S(1)}, bf16[192,1024]{1,0:T(8,128)(2,1)S(1)}, u32[]{:S(2)}, u32[]{:S(2)}) collective-permute-start(bf16[192,1024]{1,0:T(8,128)(2,1)S(1)} %reshape.224), channel_id=1, source_target_pairs={{0,15},{1,0},{2,1},{3,2},{4,3},{5,4},{6,5},{7,6},{8,7},{9,8},{10,9... | collective-permute-start | bytes 1179656 | tf_op jit(solution)/shard_map/ppermute | solution.py:68
  42.9 24.1 %collective-permute-start.8 = (bf16[192,1024]{1,0:T(8,128)(2,1)S(1)}, bf16[192,1024]{1,0:T(8,128)(2,1)}, u32[]{:S(2)}, u32[]{:S(2)}) collective-permute-start(bf16[192,1024]{1,0:T(8,128)(2,1)S(1)} %reshape.226), channel_id=1, source_target_pairs={{0,1},{1,2},{2,3},{3,4},{4,5},{5,6},{6,7},{7,8},{8,9},{9,10},{10,1... | collective-permute-start | bytes 1179656 | tf_op jit(solution)/shard_map/ppermute | solution.py:68
  44.8 15.8 %collective-permute-start.1 = (bf16[192,1024]{1,0:T(8,128)(2,1)S(1)}, bf16[192,1024]{1,0:T(8,128)(2,1)S(1)}, u32[]{:S(2)}, u32[]{:S(2)}) collective-permute-start(bf16[192,1024]{1,0:T(8,128)(2,1)S(1)} %reshape.226), channel_id=1, source_target_pairs={{0,15},{1,0},{2,1},{3,2},{4,3},{5,4},{6,5},{7,6},{8,7},{9,8},{10,9... | collective-permute-start | bytes 1179656 | tf_op jit(solution)/shard_map/ppermute | solution.py:68
  52.9 24.9 %collective-permute-start.7 = (bf16[192,1024]{1,0:T(8,128)(2,1)}, bf16[192,1024]{1,0:T(8,128)(2,1)S(1)}, u32[]{:S(2)}, u32[]{:S(2)}) collective-permute-start(bf16[192,1024]{1,0:T(8,128)(2,1)} %collective-permute-done.6), channel_id=1, source_target_pairs={{0,1},{1,2},{2,3},{3,4},{4,5},{5,6},{6,7},{7,8},{8,9},{9,10},{10,1... | collective-permute-start | bytes 1179656 | tf_op jit(solution)/shard_map/ppermute | solution.py:68
  54.8 14.6 %collective-permute-start.2 = (bf16[192,1024]{1,0:T(8,128)(2,1)S(1)}, bf16[192,1024]{1,0:T(8,128)(2,1)S(1)}, u32[]{:S(2)}, u32[]{:S(2)}) collective-permute-start(bf16[192,1024]{1,0:T(8,128)(2,1)S(1)} %collective-permute-done), channel_id=1, source_target_pairs={{0,15},{1,0},{2,1},{3,2},{4,3},{5,4},{6,5},{7,6},{8,7},{9,8},{10,9... | collective-permute-start | bytes 1179656 | tf_op jit(solution)/shard_map/ppermute | solution.py:68
  60.7 16.9 %collective-permute-start.3 = (bf16[192,1024]{1,0:T(8,128)(2,1)S(1)}, bf16[192,1024]{1,0:T(8,128)(2,1)S(1)}, u32[]{:S(2)}, u32[]{:S(2)}) collective-permute-start(bf16[192,1024]{1,0:T(8,128)(2,1)S(1)} %collective-permute-done.1), channel_id=1, source_target_pairs={{0,15},{1,0},{2,1},{3,2},{4,3},{5,4},{6,5},{7,6},{8,7},{9,8},{10,9... | collective-permute-start | bytes 1179656 | tf_op jit(solution)/shard_map/ppermute | solution.py:68
  67.1 14.2 %collective-permute-start.9 = (bf16[192,1024]{1,0:T(8,128)(2,1)}, bf16[192,1024]{1,0:T(8,128)(2,1)S(1)}, u32[]{:S(2)}, u32[]{:S(2)}) collective-permute-start(bf16[192,1024]{1,0:T(8,128)(2,1)} %collective-permute-done.8), channel_id=1, source_target_pairs={{0,1},{1,2},{2,3},{3,4},{4,5},{5,6},{6,7},{7,8},{8,9},{9,10},{10,1... | collective-permute-start | bytes 1179656 | tf_op jit(solution)/shard_map/ppermute | solution.py:68
  81.9 23.4 %collective-permute-start.10 = (bf16[192,1024]{1,0:T(8,128)(2,1)S(1)}, bf16[192,1024]{1,0:T(8,128)(2,1)S(1)}, u32[]{:S(2)}, u32[]{:S(2)}) collective-permute-start(bf16[192,1024]{1,0:T(8,128)(2,1)S(1)} %collective-permute-done.7), channel_id=1, source_target_pairs={{0,1},{1,2},{2,3},{3,4},{4,5},{5,6},{6,7},{7,8},{8,9},{9,10},{10,1... | collective-permute-start | bytes 1179656 | tf_op jit(solution)/shard_map/ppermute | solution.py:68
  83.8 14.3 %collective-permute-start.4 = (bf16[192,1024]{1,0:T(8,128)(2,1)S(1)}, bf16[192,1024]{1,0:T(8,128)(2,1)S(1)}, u32[]{:S(2)}, u32[]{:S(2)}) collective-permute-start(bf16[192,1024]{1,0:T(8,128)(2,1)S(1)} %collective-permute-done.2), channel_id=1, source_target_pairs={{0,15},{1,0},{2,1},{3,2},{4,3},{5,4},{6,5},{7,6},{8,7},{9,8},{10,9... | collective-permute-start | bytes 1179656 | tf_op jit(solution)/shard_map/ppermute | solution.py:68
  88.9 18.9 %collective-permute-start.11 = (bf16[192,1024]{1,0:T(8,128)(2,1)S(1)}, bf16[192,1024]{1,0:T(8,128)(2,1)S(1)}, u32[]{:S(2)}, u32[]{:S(2)}) collective-permute-start(bf16[192,1024]{1,0:T(8,128)(2,1)S(1)} %collective-permute-done.9), channel_id=1, source_target_pairs={{0,1},{1,2},{2,3},{3,4},{4,5},{5,6},{6,7},{7,8},{8,9},{9,10},{10,1... | collective-permute-start | bytes 1179656 | tf_op jit(solution)/shard_map/ppermute | solution.py:68
  90.9 13.7 %collective-permute-start.5 = (bf16[192,1024]{1,0:T(8,128)(2,1)S(1)}, bf16[192,1024]{1,0:T(8,128)(2,1)S(1)}, u32[]{:S(2)}, u32[]{:S(2)}) collective-permute-start(bf16[192,1024]{1,0:T(8,128)(2,1)S(1)} %collective-permute-done.3), channel_id=1, source_target_pairs={{0,15},{1,0},{2,1},{3,2},{4,3},{5,4},{6,5},{7,6},{8,7},{9,8},{10,9... | collective-permute-start | bytes 1179656 | tf_op jit(solution)/shard_map/ppermute | solution.py:68
  105.2 15.6 %collective-permute-start.12 = (bf16[192,1024]{1,0:T(8,128)(2,1)S(1)}, bf16[192,1024]{1,0:T(8,128)(2,1)S(1)}, u32[]{:S(2)}, u32[]{:S(2)}) collective-permute-start(bf16[192,1024]{1,0:T(8,128)(2,1)S(1)} %collective-permute-done.10), channel_id=1, source_target_pairs={{0,1},{1,2},{2,3},{3,4},{4,5},{5,6},{6,7},{7,8},{8,9},{9,10},{10,1... | collective-permute-start | bytes 1179656 | tf_op jit(solution)/shard_map/ppermute | solution.py:68
  107.8 18.9 %collective-permute-start.13 = (bf16[192,1024]{1,0:T(8,128)(2,1)S(1)}, bf16[192,1024]{1,0:T(8,128)(2,1)S(1)}, u32[]{:S(2)}, u32[]{:S(2)}) collective-permute-start(bf16[192,1024]{1,0:T(8,128)(2,1)S(1)} %collective-permute-done.11), channel_id=1, source_target_pairs={{0,1},{1,2},{2,3},{3,4},{4,5},{5,6},{6,7},{7,8},{8,9},{9,10},{10,1... | collective-permute-start | bytes 1179656 | tf_op jit(solution)/shard_map/ppermute | solution.py:68
  110.4 16.5 %collective-permute-start.14 = (bf16[192,1024]{1,0:T(8,128)(2,1)S(1)}, bf16[192,1024]{1,0:T(8,128)(2,1)S(1)}, u32[]{:S(2)}, u32[]{:S(2)}) collective-permute-start(bf16[192,1024]{1,0:T(8,128)(2,1)S(1)} %collective-permute-done.4), channel_id=1, source_target_pairs={{0,15},{1,0},{2,1},{3,2},{4,3},{5,4},{6,5},{7,6},{8,7},{9,8},{10,9... | collective-permute-start | bytes 1179656 | tf_op jit(solution)/shard_map/ppermute | solution.py:68
  116.2 14.9 %collective-permute-start.15 = (bf16[192,1024]{1,0:T(8,128)(2,1)S(1)}, bf16[192,1024]{1,0:T(8,128)(2,1)S(1)}, u32[]{:S(2)}, u32[]{:S(2)}) collective-permute-start(bf16[192,1024]{1,0:T(8,128)(2,1)S(1)} %collective-permute-done.5), channel_id=1, source_target_pairs={{0,15},{1,0},{2,1},{3,2},{4,3},{5,4},{6,5},{7,6},{8,7},{9,8},{10,9... | collective-permute-start | bytes 1179656 | tf_op jit(solution)/shard_map/ppermute | solution.py:68
  134.3 24.5 %all-to-all-start.2 = ((f32[16,3,384]{2,1,0:T(4,128)}), f32[16,3,384]{2,1,0:T(4,128)S(1)}, u32[]{:S(2)}, u32[]{:S(2)}) async-start(f32[16,3,384]{2,1,0:T(4,128)} %constant_dynamic-slice_fusion.1), calls=%async_computation.2 | async-start | bytes 196608 | tf_op jit(solution)/shard_map/all_to_all | solution.py:133
  143.7 10.3 %collective-permute-start.17 = (f32[1,384]{1,0:T(1,128)S(1)}, f32[1,384]{1,0:T(1,128)S(1)}, u32[]{:S(2)}, u32[]{:S(2)}) collective-permute-start(f32[1,384]{1,0:T(1,128)S(1)} %stack.228), channel_id=1, source_target_pairs={{0,3},{1,4},{2,5},{3,6},{4,7},{5,8},{6,9},{7,10},{8,11},{9,12},{10... | collective-permute-start | bytes 4616 | tf_op jit(solution)/shard_map/ppermute | solution.py:68
  149.4 9.4 %collective-permute-start.16 = (f32[2,384]{1,0:T(2,128)S(1)}, f32[2,384]{1,0:T(2,128)S(1)}, u32[]{:S(2)}, u32[]{:S(2)}) collective-permute-start(f32[2,384]{1,0:T(2,128)S(1)} %pad_maximum_fusion), channel_id=1, source_target_pairs={{0,12},{1,13},{2,14},{3,15},{4,0},{5,1},{6,2},{7,3},{8,4},{9,5},{1... | collective-permute-start | bytes 9224 | tf_op jit(solution)/shard_map/ppermute | solution.py:68
